TPU v7x, 32 devices: a whole 2x2x4 slice. The times are simulated.
32 devices in a mesh: row: 8 (over z, x), col: 4 (over y, core).
Axes of the slice: x: 2, y: 2, z: 4, core: 2. Of those that a mesh axis runs over, the one named last changes fastest.
Arguments:
- probe: float32 [32768, 128], P(('row', 'col'))
- self_weight: float32 [32768], P('row'), may hold values from 1.5 to 3
- blocks: float32 [4096, 128, 128], P(('row', 'col')), may hold values from -0.078125 to 0.078125
- block_row: int32 [4096], P(('row', 'col')), may hold values from 0 to 31
- block_col: int32 [4096], P(('row', 'col')), may hold values from 0 to 63
- counts: int32 [32], P(('row', 'col')), may hold values from 1 to 128, as said below
Outputs:
- projected: float32 [32768, 128], P(('row', 'col'))
- basis: float32 [32768, 128], P(('row', 'col'))
Inputs may be any that keep to these rules, and one draw needn't show every extreme that they name: Slots 0 to counts[g] - 1 of group g are live, the rest hold values that do not count; in every draw some group has all 128 slots live.
All inputs are finite; a program needn't handle non-finite values.
Results may differ from a plain program's by a relative error of at most 0.0001.
Values sent between devices are 32-bit elements; how exact they have to be, the bound alone decides.
No kernel may reach another device: no remote copies, remote signals or barrier semaphores. Data moves between devices by JAX's collectives and lax.ppermute only.
A program may use at most 128 MiB of HBM per device.

v0:
```python
import math

import jax
import jax.numpy as jnp
from jax import lax
from jax.experimental import pallas as pl
from jax.experimental.pallas import tpu as pltpu
from jax.sharding import PartitionSpec as P

PRECISE = lax.Precision.HIGHEST
INTERPRET = False


def shift_pairs(n, k):
    return [(i, (i + k) % n) for i in range(n)]


def ring_gather(x, axis, n):
    me = lax.axis_index(axis)
    parts = [x] + [lax.ppermute(x, axis, shift_pairs(n, -k)) for k in range(1, n)]
    return jnp.roll(jnp.stack(parts), me, axis=0).reshape(n * x.shape[0], *x.shape[1:])


def ring_reduce_scatter(x, axis, n):
    me = lax.axis_index(axis)
    chunks = x.reshape(n, x.shape[0] // n, *x.shape[1:])
    total = lax.dynamic_index_in_dim(chunks, me, 0, keepdims=False)
    for k in range(1, n):
        send = lax.dynamic_index_in_dim(chunks, (me + k) % n, 0, keepdims=False)
        total = total + lax.ppermute(send, axis, shift_pairs(n, k))
    return total


def butterfly_sum(x, axes, n):
    if n & (n - 1):
        return lax.psum(x, axes)
    step = 1
    while step < n:
        x = x + lax.ppermute(x, axes, [(i, i ^ step) for i in range(n)])
        step *= 2
    return x


def slot_product(blocks, source, block_row, block_col, counts, out_rows, transpose):
    slot_count, block_size = blocks.shape[0], blocks.shape[1]
    width = source.shape[1]
    group = 8 if slot_count % 8 == 0 else 1

    def kernel(row_ref, col_ref, count_ref, block_ref, source_ref, out_ref):
        step = pl.program_id(0)

        @pl.when(step == 0)
        def _():
            out_ref[...] = jnp.zeros_like(out_ref)

        def body(s, carry):
            slot = step * group + s
            read = row_ref[slot] if transpose else col_ref[slot]
            write = col_ref[slot] if transpose else row_ref[slot]

            @pl.when(slot < count_ref[0])
            def _():
                piece = source_ref[pl.ds(pl.multiple_of(read * block_size, block_size), block_size), :]
                block = block_ref[s]
                if transpose:
                    block = block.T
                product = jnp.dot(
                    block, piece, precision=PRECISE, preferred_element_type=jnp.float32
                )
                at = pl.ds(pl.multiple_of(write * block_size, block_size), block_size)
                out_ref[at, :] = out_ref[at, :] + product

            return carry

        lax.fori_loop(0, group, body, 0, unroll=True)

    grid_spec = pltpu.PrefetchScalarGridSpec(
        num_scalar_prefetch=3,
        grid=(slot_count // group,),
        in_specs=[
            pl.BlockSpec((group, block_size, block_size), lambda g, *_: (g, 0, 0)),
            pl.BlockSpec(source.shape, lambda g, *_: (0, 0)),
        ],
        out_specs=pl.BlockSpec((out_rows, width), lambda g, *_: (0, 0)),
    )
    return pl.pallas_call(
        kernel,
        grid_spec=grid_spec,
        out_shape=jax.ShapeDtypeStruct((out_rows, width), jnp.float32),
        compiler_params=pltpu.CompilerParams(
            dimension_semantics=("arbitrary",), vmem_limit_bytes=48 * 1024 * 1024
        ),
        interpret=INTERPRET,
    )(block_row, block_col, counts, blocks, source)


def shards(probe, self_weight, blocks, block_row, block_col, counts):
    col_count = lax.axis_size("col")
    row_count = lax.axis_size("row")
    block_size = blocks.shape[1]
    probe_width = probe.shape[1]
    slot_count = blocks.shape[0]
    local_rows = probe.shape[0]
    owner_rows = local_rows * col_count
    owner_blocks = owner_rows // block_size
    stripe_rows = local_rows * row_count
    stripe_blocks = stripe_rows // block_size
    answers = local_rows * row_count * col_count
    stripe_probe = lax.all_gather(probe, "row", axis=0, tiled=True)
    partial_value = slot_product(
        blocks, stripe_probe, block_row, block_col, counts, owner_rows, False
    )
    local_start = lax.axis_index("col") * local_rows
    local_weight = lax.dynamic_slice_in_dim(self_weight, local_start, local_rows, 0)
    share_sum = ring_reduce_scatter(partial_value, "col", col_count)
    projected = local_weight[:, None] * probe + share_sum
    owner_y = ring_gather(projected, "col", col_count)
    w_partial = slot_product(blocks, owner_y, block_row, block_col, counts, stripe_rows, True)
    w_share = lax.psum_scatter(w_partial, "row", scatter_dimension=0, tiled=True)
    sketch = local_weight[:, None] * projected + w_share
    gram_part = jnp.dot(sketch.T, sketch, precision=PRECISE, preferred_element_type=jnp.float32)
    gram = butterfly_sum(gram_part, ("row", "col"), row_count * col_count)
    lower = jnp.linalg.cholesky(gram)
    solved = lax.linalg.triangular_solve(
        lower, sketch, left_side=False, lower=True, transpose_a=True
    )
    basis = solved * math.sqrt(answers)
    return (projected, basis)


def solution(mesh):
    in_specs = (
        P(("row", "col"), None),
        P("row"),
        P(("row", "col"), None, None),
        P(("row", "col")),
        P(("row", "col")),
        P(("row", "col")),
    )
    out_specs = (P(("row", "col"), None), P(("row", "col"), None))
    return jax.shard_map(shards, mesh=mesh, in_specs=in_specs, out_specs=out_specs, check_vma=False)
```

profile of v0, /device:TPU:0, one launch (start us, length us, event | category | flops | bytes accessed | tf_op | source)
XLA Modules:
  0.0 354.8 jit_solution(15379252763807229834)
XLA Ops:
  8.6 77.0 %all-gather.2.cloned.1.call-done.source_ref = f32[8192,128]{1,0:T(8,128)} async-done(((f32[1024,128]{1,0:T(8,128)}), f32[8192,128]{1,0:T(8,128)}) %all-gather.2.cloned.1.call-update) | async-done | bytes 4194320 | tf_op jit(solution)/shard_map/all_gather | solution.py:109
  87.0 17.2 %shard_map.77 = f32[4096,128]{1,0:T(8,128)S(1)} custom-call(s32[128]{0:T(128)S(1)} %copy-done, s32[128]{0:T(128)S(1)} %copy-done.2, s32[1]{0:T(128)S(6)} %copy.19.count_ref, f32[128,128,128]{2,1,0:T(8,128)} %block_ref.3, f32[8192,128]{1,0:T(8,128)} %all-gather.2.cloned.1.call-done.source_ref), custom_call_target="tpu_custom_call" | custom-call | tf_op jit(solution)/shard_map/pallas_call | solution.py:86
  105.4 12.2 %collective-permute-start.2 = (f32[1024,128]{1,0:T(8,128)}, f32[1024,128]{1,0:T(8,128)}, u32[]{:S(2)}, u32[]{:S(2)}) collective-permute-start(f32[1024,128]{1,0:T(8,128)} %get-tuple-element.5), channel_id=1, source_target_pairs={{0,3},{1,0},{2,1},{3,2},{4,7},{5,4},{6,5},{7,6},{8,11},{9,8},{10,9... | collective-permute-start | bytes 1572872 | tf_op jit(solution)/shard_map/ppermute | solution.py:30
  118.6 10.9 %collective-permute-done = f32[1024,128]{1,0:T(8,128)S(1)} collective-permute-done((f32[1024,128]{1,0:T(8,128)}, f32[1024,128]{1,0:T(8,128)S(1)}, u32[]{:S(2)}, u32[]{:S(2)}) %collective-permute-start) | collective-permute-done | bytes 524320 | tf_op jit(solution)/shard_map/ppermute | solution.py:30
  130.3 11.2 %collective-permute-done.1 = f32[1024,128]{1,0:T(8,128)} collective-permute-done((f32[1024,128]{1,0:T(8,128)}, f32[1024,128]{1,0:T(8,128)}, u32[]{:S(2)}, u32[]{:S(2)}) %collective-permute-start.1) | collective-permute-done | bytes 524320 | tf_op jit(solution)/shard_map/ppermute | solution.py:30
  141.6 2.4 bitcast_dynamic-update-slice_fusion.6
  145.0 11.3 %collective-permute-done.3 = f32[1024,128]{1,0:T(8,128)S(1)} collective-permute-done((f32[1024,128]{1,0:T(8,128)S(1)}, f32[1024,128]{1,0:T(8,128)S(1)}, u32[]{:S(2)}, u32[]{:S(2)}) %collective-permute-start.3) | collective-permute-done | bytes 524320 | tf_op jit(solution)/shard_map/ppermute | solution.py:20
  157.1 11.4 %collective-permute-done.4 = f32[1024,128]{1,0:T(8,128)S(1)} collective-permute-done((f32[1024,128]{1,0:T(8,128)S(1)}, f32[1024,128]{1,0:T(8,128)S(1)}, u32[]{:S(2)}, u32[]{:S(2)}) %collective-permute-start.4) | collective-permute-done | bytes 524320 | tf_op jit(solution)/shard_map/ppermute | solution.py:20
  173.5 1.7 constant_dynamic-slice_fusion
  175.3 20.4 %shard_map.78 = f32[8192,128]{1,0:T(8,128)} custom-call(s32[128]{0:T(128)S(1)} %copy-done.1, s32[128]{0:T(128)S(1)} %copy-done.3, s32[1]{0:T(128)S(6)} %copy.19.count_ref, f32[128,128,128]{2,1,0:T(8,128)} %block_ref.3, f32[4096,128]{1,0:T(8,128)S(1)} %bitcast.40), custom_call_target="tpu_custom_call" | custom-call | tf_op jit(solution)/shard_map/pallas_call | solution.py:86
  195.7 104.7 %reduce-scatter.2.cloned.1.call-done = f32[1024,128]{1,0:T(8,128)} async-done(((f32[8192,128]{1,0:T(8,128)}), f32[1024,128]{1,0:T(8,128)}) %reduce-scatter.2.cloned.1.call-update) | async-done | bytes 524304 | tf_op jit(solution)/shard_map/reduce_scatter | solution.py:119
  300.4 2.5 fusion.3
  303.0 1.2 collective-permute-done.6
  304.2 1.5 collective-permute-start.7
  305.8 2.8 collective-permute-done.7
  308.6 1.5 collective-permute-start.8
  310.1 2.8 collective-permute-done.8
  312.9 1.8 collective-permute-start.9
  314.7 2.6 collective-permute-done.9
  317.3 2.2 collective-permute-start.10
  319.5 3.0 collective-permute-done.10
  322.6 11.7 %cholesky.16 = f32[128,128]{1,0:T(8,128)S(1)} custom-call(f32[128,128]{1,0:T(8,128)S(1)} %fusion.6), custom_call_target="Cholesky" | custom-call | tf_op jit(solution)/shard_map/jit(cholesky)/cholesky | solution.py:123
  335.7 9.8 %custom-call.6 = f32[1,128,128]{1,2,0:T(8,128)S(1)} custom-call(f32[1,128,128]{2,1,0:T(8,128)S(1)} %fusion.4), custom_call_target="InvertDiagBlocksLowerTriangular" | custom-call | tf_op jit(solution)/shard_map/triangular_solve | solution.py:124
  345.5 2.5 convolution_multiply_fusion
  (45 shorter events, 13.7 us)
Async XLA Ops:
  7.2 78.5 %all-gather.2.cloned.1.call-start = ((), (), s32[]{:S(2)}) async-start(), calls=%async_computation.1 | async-start | bytes 4718592 | tf_op jit(solution)/shard_map/all_gather | solution.py:109
  7.9 292.5 %reduce-scatter.2.cloned.1.call-start = ((), (), s32[]{:S(2)}) async-start(), calls=%async_computation.2 | async-start | bytes 4718592 | tf_op jit(solution)/shard_map/reduce_scatter | solution.py:119
  85.6 0.7 copy-start
  86.3 0.7 copy-start.2
  87.0 54.6 %copy-start.5 = (f32[1024,128]{1,0:T(8,128)S(1)}, f32[1024,128]{1,0:T(8,128)}, u32[]{:S(2)}) copy-start(f32[1024,128]{1,0:T(8,128)} %param.6) | copy-start | bytes 1572868
  105.4 24.2 %collective-permute-start = (f32[1024,128]{1,0:T(8,128)}, f32[1024,128]{1,0:T(8,128)S(1)}, u32[]{:S(2)}, u32[]{:S(2)}) collective-permute-start(f32[1024,128]{1,0:T(8,128)} %get-tuple-element.4), channel_id=1, source_target_pairs={{0,1},{1,2},{2,3},{3,0},{4,5},{5,6},{6,7},{7,4},{8,9},{9,10},{10,1... | collective-permute-start | bytes 1572872 | tf_op jit(solution)/shard_map/ppermute | solution.py:30
  105.4 24.7 %collective-permute-start.2 = (f32[1024,128]{1,0:T(8,128)}, f32[1024,128]{1,0:T(8,128)}, u32[]{:S(2)}, u32[]{:S(2)}) collective-permute-start(f32[1024,128]{1,0:T(8,128)} %get-tuple-element.5), channel_id=1, source_target_pairs={{0,3},{1,0},{2,1},{3,2},{4,7},{5,4},{6,5},{7,6},{8,11},{9,8},{10,9... | collective-permute-start | bytes 1572872 | tf_op jit(solution)/shard_map/ppermute | solution.py:30
  117.5 24.0 %collective-permute-start.1 = (f32[1024,128]{1,0:T(8,128)}, f32[1024,128]{1,0:T(8,128)}, u32[]{:S(2)}, u32[]{:S(2)}) collective-permute-start(f32[1024,128]{1,0:T(8,128)} %get-tuple-element.6), channel_id=1, source_target_pairs={{0,2},{1,3},{2,0},{3,1},{4,6},{5,7},{6,4},{7,5},{8,10},{9,11},{10,... | collective-permute-start | bytes 1572872 | tf_op jit(solution)/shard_map/ppermute | solution.py:30
  129.5 0.8 copy-start.6
  143.9 201.6 %copy-start.4 = (f32[1024,128]{1,0:T(8,128)}, f32[1024,128]{1,0:T(8,128)S(1)}, u32[]{:S(2)}) copy-start(f32[1024,128]{1,0:T(8,128)S(1)} %get-tuple-element.3) | copy-start | bytes 1572868
  143.9 12.3 %collective-permute-start.3 = (f32[1024,128]{1,0:T(8,128)S(1)}, f32[1024,128]{1,0:T(8,128)S(1)}, u32[]{:S(2)}, u32[]{:S(2)}) collective-permute-start(f32[1024,128]{1,0:T(8,128)S(1)} %get-tuple-element.3), channel_id=1, source_target_pairs={{0,3},{1,0},{2,1},{3,2},{4,7},{5,4},{6,5},{7,6},{8,11},{9,8},{10,9... | collective-permute-start | bytes 1572872 | tf_op jit(solution)/shard_map/ppermute | solution.py:20
  143.9 24.5 %collective-permute-start.4 = (f32[1024,128]{1,0:T(8,128)S(1)}, f32[1024,128]{1,0:T(8,128)S(1)}, u32[]{:S(2)}, u32[]{:S(2)}) collective-permute-start(f32[1024,128]{1,0:T(8,128)S(1)} %get-tuple-element.3), channel_id=1, source_target_pairs={{0,2},{1,3},{2,0},{3,1},{4,6},{5,7},{6,4},{7,5},{8,10},{9,11},{10,... | collective-permute-start | bytes 1572872 | tf_op jit(solution)/shard_map/ppermute | solution.py:20
  145.0 24.3 %collective-permute-start.5 = (f32[1024,128]{1,0:T(8,128)S(1)}, f32[1024,128]{1,0:T(8,128)S(1)}, u32[]{:S(2)}, u32[]{:S(2)}) collective-permute-start(f32[1024,128]{1,0:T(8,128)S(1)} %get-tuple-element.3), channel_id=1, source_target_pairs={{0,1},{1,2},{2,3},{3,0},{4,5},{5,6},{6,7},{7,4},{8,9},{9,10},{10,1... | collective-permute-start | bytes 1572872 | tf_op jit(solution)/shard_map/ppermute | solution.py:20
  170.2 5.1 %copy-start.1 = (s32[128]{0:T(128)S(1)}, s32[128]{0:T(128)}, u32[]{:S(2)}) copy-start(s32[128]{0:T(128)} %row_ref.3) | copy-start | bytes 1540
  170.2 5.1 %copy-start.3 = (s32[128]{0:T(128)S(1)}, s32[128]{0:T(128)}, u32[]{:S(2)}) copy-start(s32[128]{0:T(128)} %col_ref.3) | copy-start | bytes 1540
  302.9 1.3 collective-permute-start.6
  304.2 4.3 %collective-permute-start.7 = (f32[128,128]{0,1:T(8,128)S(1)}, f32[128,128]{0,1:T(8,128)S(1)}, u32[]{:S(2)}, u32[]{:S(2)}) collective-permute-start(f32[128,128]{0,1:T(8,128)S(1)} %add.106), channel_id=1, source_target_pairs={{0,2},{1,3},{2,0},{3,1},{4,6},{5,7},{6,4},{7,5},{8,10},{9,11},{10,... | collective-permute-start | bytes 196616 | tf_op jit(solution)/shard_map/ppermute | solution.py:39
  308.6 4.3 %collective-permute-start.8 = (f32[128,128]{0,1:T(8,128)S(1)}, f32[128,128]{0,1:T(8,128)S(1)}, u32[]{:S(2)}, u32[]{:S(2)}) collective-permute-start(f32[128,128]{0,1:T(8,128)S(1)} %add.107), channel_id=1, source_target_pairs={{0,4},{1,5},{2,6},{3,7},{4,0},{5,1},{6,2},{7,3},{8,12},{9,13},{10,... | collective-permute-start | bytes 196616 | tf_op jit(solution)/shard_map/ppermute | solution.py:39
  312.9 4.3 %collective-permute-start.9 = (f32[128,128]{0,1:T(8,128)S(1)}, f32[128,128]{0,1:T(8,128)S(1)}, u32[]{:S(2)}, u32[]{:S(2)}) collective-permute-start(f32[128,128]{0,1:T(8,128)S(1)} %add.108), channel_id=1, source_target_pairs={{0,8},{1,9},{2,10},{3,11},{4,12},{5,13},{6,14},{7,15},{8,0},{9,1},... | collective-permute-start | bytes 196616 | tf_op jit(solution)/shard_map/ppermute | solution.py:39
  317.3 5.2 %collective-permute-start.10 = (f32[128,128]{0,1:T(8,128)S(1)}, f32[128,128]{0,1:T(8,128)S(1)}, u32[]{:S(2)}, u32[]{:S(2)}) collective-permute-start(f32[128,128]{0,1:T(8,128)S(1)} %add.109), channel_id=1, source_target_pairs={{0,16},{1,17},{2,18},{3,19},{4,20},{5,21},{6,22},{7,23},{8,24},{9,... | collective-permute-start | bytes 196616 | tf_op jit(solution)/shard_map/ppermute | solution.py:39
Sparse Core Ops, SparseCore 0:
  10.1 75.4 all-gather.1
  195.8 104.5 reduce-scatter.1
where the time goes:
time: 355 us
  waiting for transfers between devices  240 us (68%)
  Pallas kernels  37.6 us (11%)
  other arithmetic  25.3 us (7%)
  starting transfers between devices  20.8 us (6%)
  between operations  14.8 us (4%)
  local copies, waits for them, and re-layouts  11.1 us (3%)
  matrix products  4.96 us (1%)
    reduce_scatter x1, waiting for transfers between devices, shards(): lax.psum_scatter(w_partial, 'row', scatter_dimension=0, tiled=True)  105 us
    all_gather x1, waiting for transfers between devices, shards(): stripe_probe = lax.all_gather(probe, 'row', axis=0, tiled=True)  77 us
    pallas_call x2, Pallas kernels, slot_product(): pl.pallas_call(kernel, grid_spec=grid_spec, out_shape=jax.ShapeDtypeStruc...  37.6 us
    ppermute x3, waiting for transfers between devices, ring_reduce_scatter(): total = total + lax.ppermute(send, axis, shift_pairs(n, k))  22.7 us
    ppermute x3, waiting for transfers between devices, ring_gather(): lax.ppermute(x, axis, shift_pairs(n, -k))  22.6 us
    ppermute x3, starting transfers between devices, ring_reduce_scatter(): total = total + lax.ppermute(send, axis, shift_pairs(n, k))  12.6 us
    ppermute x5, waiting for transfers between devices, butterfly_sum(): x = x + lax.ppermute(x, axes, [(i, i ^ step) for i in range(n)])  12.4 us
    another operation x3, other arithmetic, shards(): lower = jnp.linalg.cholesky(gram)  12.4 us
  transfers between devices with their start and end apart: 13, of which 12 were waited for; matrix products, arithmetic and copies ran while one was open for 1% of the time, Pallas kernels for 0%

commit v1 on v0

--- a/solution.py
+++ b/solution.py
@@ -29,6 +29,12 @@
         send = lax.dynamic_index_in_dim(chunks, (me + k) % n, 0, keepdims=False)
         total = total + lax.ppermute(send, axis, shift_pairs(n, k))
     return total
+
+
+def group_sum(x, axis, n):
+    me = lax.axis_index(axis)
+    parts = [x] + [lax.ppermute(x, axis, shift_pairs(n, -k)) for k in range(1, n)]
+    return jnp.sum(jnp.roll(jnp.stack(parts), me, axis=0), axis=0)
 
 
 def butterfly_sum(x, axes, n):
@@ -119,7 +125,7 @@
     w_share = lax.psum_scatter(w_partial, "row", scatter_dimension=0, tiled=True)
     sketch = local_weight[:, None] * projected + w_share
     gram_part = jnp.dot(sketch.T, sketch, precision=PRECISE, preferred_element_type=jnp.float32)
-    gram = butterfly_sum(gram_part, ("row", "col"), row_count * col_count)
+    gram = group_sum(group_sum(gram_part, "col", col_count), "row", row_count)
     lower = jnp.linalg.cholesky(gram)
     solved = lax.linalg.triangular_solve(
         lower, sketch, left_side=False, lower=True, transpose_a=True

time: 355 us -> 363 us (1.023)
  starting transfers between devices: 20.8 us -> 33.8 us
  Pallas kernels: 37.6 us -> 31.8 us
    ppermute x5 -> x10, starting transfers between devices: 7.14 us -> 15.8 us  [group_sum(): lax.ppermute(x, axis, shift_pairs(n, -k))]
    pallas_call x2, Pallas kernels: 37.6 us -> 31.8 us  [slot_product(): pl.pallas_call(kernel, grid_spec=grid_spec, out_shape=jax.ShapeDtypeStruc...]
    reduce_scatter x1, waiting for transfers between devices: 105 us -> 110 us  [shards(): lax.psum_scatter(w_partial, 'row', scatter_dimension=0, tiled=True)]
    ppermute x5 -> x10, waiting for transfers between devices: 12.4 us -> 11.4 us  [group_sum(): lax.ppermute(x, axis, shift_pairs(n, -k))]
  transfers between devices with their start and end apart: 13 -> 18, of which waited for: 12 -> 11; matrix products, arithmetic and copies ran while one was open for 1% -> 1% of each run, Pallas kernels for 0% -> 0%
where the time goes in v1:
time: 363 us
  waiting for transfers between devices  243 us (67%)
  starting transfers between devices  33.8 us (9%)
  Pallas kernels  31.8 us (9%)
  other arithmetic  25.3 us (7%)
  between operations  15 us (4%)
  local copies, waits for them, and re-layouts  11.1 us (3%)
  matrix products  3.98 us (1%)
    reduce_scatter x1, waiting for transfers between devices, shards(): lax.psum_scatter(w_partial, 'row', scatter_dimension=0, tiled=True)  110 us
    all_gather x1, waiting for transfers between devices, shards(): stripe_probe = lax.all_gather(probe, 'row', axis=0, tiled=True)  77 us
    pallas_call x2, Pallas kernels, slot_product(): pl.pallas_call(kernel, grid_spec=grid_spec, out_shape=jax.ShapeDtypeStruc...  31.8 us
    ppermute x3, waiting for transfers between devices, ring_gather(): lax.ppermute(x, axis, shift_pairs(n, -k))  22.8 us
    ppermute x3, waiting for transfers between devices, ring_reduce_scatter(): total = total + lax.ppermute(send, axis, shift_pairs(n, k))  20.9 us
    ppermute x10, starting transfers between devices, group_sum(): lax.ppermute(x, axis, shift_pairs(n, -k))  15.8 us
    ppermute x3, starting transfers between devices, ring_reduce_scatter(): total = total + lax.ppermute(send, axis, shift_pairs(n, k))  15.2 us
    another operation x3, other arithmetic, shards(): lower = jnp.linalg.cholesky(gram)  12.4 us
  transfers between devices with their start and end apart: 18, of which 11 were waited for; matrix products, arithmetic and copies ran while one was open for 1% of the time, Pallas kernels for 0%

profile of v1, /device:TPU:0, one launch (start us, length us, event | category | flops | bytes accessed | tf_op | source)
XLA Modules:
  0.0 363.4 jit_solution(4100239153594625216)
XLA Ops:
  8.6 77.0 %all-gather.2.cloned.1.call-done.source_ref = f32[8192,128]{1,0:T(8,128)} async-done(((f32[1024,128]{1,0:T(8,128)}), f32[8192,128]{1,0:T(8,128)}) %all-gather.2.cloned.1.call-update) | async-done | bytes 4194320 | tf_op jit(solution)/shard_map/all_gather | solution.py:115
  87.0 14.8 %shard_map.77 = f32[4096,128]{1,0:T(8,128)S(1)} custom-call(s32[128]{0:T(128)S(1)} %copy-done, s32[128]{0:T(128)S(1)} %copy-done.2, s32[1]{0:T(128)S(6)} %copy.39.count_ref, f32[128,128,128]{2,1,0:T(8,128)} %block_ref.3, f32[8192,128]{1,0:T(8,128)} %all-gather.2.cloned.1.call-done.source_ref), custom_call_target="tpu_custom_call" | custom-call | tf_op jit(solution)/shard_map/pallas_call | solution.py:92
  102.9 13.5 %collective-permute-start = (f32[1024,128]{1,0:T(8,128)}, f32[1024,128]{1,0:T(8,128)S(1)}, u32[]{:S(2)}, u32[]{:S(2)}) collective-permute-start(f32[1024,128]{1,0:T(8,128)} %get-tuple-element.4), channel_id=1, source_target_pairs={{0,1},{1,2},{2,3},{3,0},{4,5},{5,6},{6,7},{7,4},{8,9},{9,10},{10,1... | collective-permute-start | bytes 1572872 | tf_op jit(solution)/shard_map/ppermute | solution.py:30
  116.5 1.6 collective-permute-start.1
  118.8 10.3 %collective-permute-done.2 = f32[1024,128]{1,0:T(8,128)} collective-permute-done((f32[1024,128]{1,0:T(8,128)}, f32[1024,128]{1,0:T(8,128)}, u32[]{:S(2)}, u32[]{:S(2)}) %collective-permute-start.2) | collective-permute-done | bytes 524320 | tf_op jit(solution)/shard_map/ppermute | solution.py:30
  129.1 10.5 %collective-permute-done.1 = f32[1024,128]{1,0:T(8,128)} collective-permute-done((f32[1024,128]{1,0:T(8,128)}, f32[1024,128]{1,0:T(8,128)}, u32[]{:S(2)}, u32[]{:S(2)}) %collective-permute-start.1) | collective-permute-done | bytes 524320 | tf_op jit(solution)/shard_map/ppermute | solution.py:30
  139.7 2.4 bitcast_dynamic-update-slice_fusion.6
  144.7 10.6 %collective-permute-done.3 = f32[1024,128]{1,0:T(8,128)S(1)} collective-permute-done((f32[1024,128]{1,0:T(8,128)S(1)}, f32[1024,128]{1,0:T(8,128)S(1)}, u32[]{:S(2)}, u32[]{:S(2)}) %collective-permute-start.3) | collective-permute-done | bytes 524320 | tf_op jit(solution)/shard_map/ppermute | solution.py:20
  156.2 12.2 %collective-permute-done.4 = f32[1024,128]{1,0:T(8,128)S(1)} collective-permute-done((f32[1024,128]{1,0:T(8,128)S(1)}, f32[1024,128]{1,0:T(8,128)S(1)}, u32[]{:S(2)}, u32[]{:S(2)}) %collective-permute-start.4) | collective-permute-done | bytes 524320 | tf_op jit(solution)/shard_map/ppermute | solution.py:20
  173.4 1.7 constant_dynamic-slice_fusion
  175.1 17.0 %shard_map.78 = f32[8192,128]{1,0:T(8,128)} custom-call(s32[128]{0:T(128)S(1)} %copy-done.1, s32[128]{0:T(128)S(1)} %copy-done.3, s32[1]{0:T(128)S(6)} %copy.39.count_ref, f32[128,128,128]{2,1,0:T(8,128)} %block_ref.3, f32[4096,128]{1,0:T(8,128)S(1)} %bitcast.76), custom_call_target="tpu_custom_call" | custom-call | tf_op jit(solution)/shard_map/pallas_call | solution.py:92
  192.1 109.8 %reduce-scatter.2.cloned.1.call-done = f32[1024,128]{1,0:T(8,128)} async-done(((f32[8192,128]{1,0:T(8,128)}), f32[1024,128]{1,0:T(8,128)}) %reduce-scatter.2.cloned.1.call-update) | async-done | bytes 524304 | tf_op jit(solution)/shard_map/reduce_scatter | solution.py:125
  301.9 2.6 constant_dynamic-update-slice_fusion.7
  307.1 2.9 collective-permute-done.7
  311.7 1.7 collective-permute-start.14
  313.4 1.5 collective-permute-start.13
  314.9 2.3 collective-permute-start.12
  317.2 2.1 collective-permute-start.9
  319.3 2.2 collective-permute-done.9
  322.8 3.0 collective-permute-done.10
  325.8 3.3 collective-permute-start.11
  329.1 2.7 collective-permute-done.11
  332.2 11.7 %cholesky.16 = f32[128,128]{1,0:T(8,128)S(1)} custom-call(f32[128,128]{1,0:T(8,128)S(1)} %fusion.6), custom_call_target="Cholesky" | custom-call | tf_op jit(solution)/shard_map/jit(cholesky)/cholesky | solution.py:129
  345.3 9.8 %custom-call.6 = f32[1,128,128]{1,2,0:T(8,128)S(1)} custom-call(f32[1,128,128]{2,1,0:T(8,128)S(1)} %fusion.4), custom_call_target="InvertDiagBlocksLowerTriangular" | custom-call | tf_op jit(solution)/shard_map/triangular_solve | solution.py:130
  (77 shorter events, 21.1 us)
Async XLA Ops:
  7.2 78.5 %all-gather.2.cloned.1.call-start = ((), (), s32[]{:S(2)}) async-start(), calls=%async_computation.1 | async-start | bytes 4718592 | tf_op jit(solution)/shard_map/all_gather | solution.py:115
  7.9 294.0 %reduce-scatter.2.cloned.1.call-start = ((), (), s32[]{:S(2)}) async-start(), calls=%async_computation.2 | async-start | bytes 4718592 | tf_op jit(solution)/shard_map/reduce_scatter | solution.py:125
  87.0 52.7 %copy-start.5 = (f32[1024,128]{1,0:T(8,128)S(1)}, f32[1024,128]{1,0:T(8,128)}, u32[]{:S(2)}) copy-start(f32[1024,128]{1,0:T(8,128)} %param.6) | copy-start | bytes 1572868
  102.9 15.9 %collective-permute-start = (f32[1024,128]{1,0:T(8,128)}, f32[1024,128]{1,0:T(8,128)S(1)}, u32[]{:S(2)}, u32[]{:S(2)}) collective-permute-start(f32[1024,128]{1,0:T(8,128)} %get-tuple-element.4), channel_id=1, source_target_pairs={{0,1},{1,2},{2,3},{3,0},{4,5},{5,6},{6,7},{7,4},{8,9},{9,10},{10,1... | collective-permute-start | bytes 1572872 | tf_op jit(solution)/shard_map/ppermute | solution.py:30
  116.5 12.6 %collective-permute-start.2 = (f32[1024,128]{1,0:T(8,128)}, f32[1024,128]{1,0:T(8,128)}, u32[]{:S(2)}, u32[]{:S(2)}) collective-permute-start(f32[1024,128]{1,0:T(8,128)} %get-tuple-element.5), channel_id=1, source_target_pairs={{0,3},{1,0},{2,1},{3,2},{4,7},{5,4},{6,5},{7,6},{8,11},{9,8},{10,9... | collective-permute-start | bytes 1572872 | tf_op jit(solution)/shard_map/ppermute | solution.py:30
  116.5 23.2 %collective-permute-start.1 = (f32[1024,128]{1,0:T(8,128)}, f32[1024,128]{1,0:T(8,128)}, u32[]{:S(2)}, u32[]{:S(2)}) collective-permute-start(f32[1024,128]{1,0:T(8,128)} %get-tuple-element.6), channel_id=1, source_target_pairs={{0,2},{1,3},{2,0},{3,1},{4,6},{5,7},{6,4},{7,5},{8,10},{9,11},{10,... | collective-permute-start | bytes 1572872 | tf_op jit(solution)/shard_map/ppermute | solution.py:30
  118.8 10.3 %copy-start.7 = (f32[1024,128]{1,0:T(8,128)}, f32[1024,128]{1,0:T(8,128)S(1)}, u32[]{:S(2)}) copy-start(f32[1024,128]{1,0:T(8,128)S(1)} %collective-permute-done) | copy-start | bytes 1572868
  142.0 213.1 %copy-start.4 = (f32[1024,128]{1,0:T(8,128)}, f32[1024,128]{1,0:T(8,128)S(1)}, u32[]{:S(2)}) copy-start(f32[1024,128]{1,0:T(8,128)S(1)} %get-tuple-element.3) | copy-start | bytes 1572868
  142.0 13.3 %collective-permute-start.3 = (f32[1024,128]{1,0:T(8,128)S(1)}, f32[1024,128]{1,0:T(8,128)S(1)}, u32[]{:S(2)}, u32[]{:S(2)}) collective-permute-start(f32[1024,128]{1,0:T(8,128)S(1)} %get-tuple-element.3), channel_id=1, source_target_pairs={{0,3},{1,0},{2,1},{3,2},{4,7},{5,4},{6,5},{7,6},{8,11},{9,8},{10,9... | collective-permute-start | bytes 1572872 | tf_op jit(solution)/shard_map/ppermute | solution.py:20
  143.5 24.8 %collective-permute-start.4 = (f32[1024,128]{1,0:T(8,128)S(1)}, f32[1024,128]{1,0:T(8,128)S(1)}, u32[]{:S(2)}, u32[]{:S(2)}) collective-permute-start(f32[1024,128]{1,0:T(8,128)S(1)} %get-tuple-element.3), channel_id=1, source_target_pairs={{0,2},{1,3},{2,0},{3,1},{4,6},{5,7},{6,4},{7,5},{8,10},{9,11},{10,... | collective-permute-start | bytes 1572872 | tf_op jit(solution)/shard_map/ppermute | solution.py:20
  144.5 24.7 %collective-permute-start.5 = (f32[1024,128]{1,0:T(8,128)S(1)}, f32[1024,128]{1,0:T(8,128)S(1)}, u32[]{:S(2)}, u32[]{:S(2)}) collective-permute-start(f32[1024,128]{1,0:T(8,128)S(1)} %get-tuple-element.3), channel_id=1, source_target_pairs={{0,1},{1,2},{2,3},{3,0},{4,5},{5,6},{6,7},{7,4},{8,9},{9,10},{10,1... | collective-permute-start | bytes 1572872 | tf_op jit(solution)/shard_map/ppermute | solution.py:20
  170.1 5.1 %copy-start.1 = (s32[128]{0:T(128)S(1)}, s32[128]{0:T(128)}, u32[]{:S(2)}) copy-start(s32[128]{0:T(128)} %row_ref.3) | copy-start | bytes 1540
  170.1 5.1 %copy-start.3 = (s32[128]{0:T(128)S(1)}, s32[128]{0:T(128)}, u32[]{:S(2)}) copy-start(s32[128]{0:T(128)} %col_ref.3) | copy-start | bytes 1540
  301.9 53.2 %copy-start.6 = (f32[1024,128]{1,0:T(8,128)S(1)}, f32[1024,128]{1,0:T(8,128)}, u32[]{:S(2)}) copy-start(f32[1024,128]{1,0:T(8,128)} %reduce-scatter.2.cloned.1.call-done) | copy-start | bytes 1572868
  304.5 2.6 collective-permute-start.6
  305.1 5.0 %collective-permute-start.8 = (f32[128,128]{1,0:T(8,128)S(1)}, f32[128,128]{1,0:T(8,128)S(1)}, u32[]{:S(2)}, u32[]{:S(2)}) collective-permute-start(f32[128,128]{1,0:T(8,128)S(1)} %get-tuple-element.8), channel_id=1, source_target_pairs={{0,1},{1,2},{2,3},{3,0},{4,5},{5,6},{6,7},{7,4},{8,9},{9,10},{10,1... | collective-permute-start | bytes 196616 | tf_op jit(solution)/shard_map/ppermute | solution.py:36
  305.1 5.0 %collective-permute-start.7 = (f32[128,128]{1,0:T(8,128)S(1)}, f32[128,128]{1,0:T(8,128)S(1)}, u32[]{:S(2)}, u32[]{:S(2)}) collective-permute-start(f32[128,128]{1,0:T(8,128)S(1)} %get-tuple-element.8), channel_id=1, source_target_pairs={{0,2},{1,3},{2,0},{3,1},{4,6},{5,7},{6,4},{7,5},{8,10},{9,11},{10,... | collective-permute-start | bytes 196616 | tf_op jit(solution)/shard_map/ppermute | solution.py:36
  310.2 21.8 %collective-permute-start.15 = (f32[128,128]{1,0:T(8,128)S(1)}, f32[128,128]{1,0:T(8,128)S(1)}, u32[]{:S(2)}, u32[]{:S(2)}) collective-permute-start(f32[128,128]{1,0:T(8,128)S(1)} %dynamic-slice_reduce_fusion.1), channel_id=1, source_target_pairs={{0,4},{4,8},{8,12},{12,16},{16,20},{20,24},{24,28},{28,0},{1,5},{5... | collective-permute-start | bytes 196616 | tf_op jit(solution)/shard_map/ppermute | solution.py:36
  311.7 20.2 %collective-permute-start.14 = (f32[128,128]{1,0:T(8,128)S(1)}, f32[128,128]{1,0:T(8,128)S(1)}, u32[]{:S(2)}, u32[]{:S(2)}) collective-permute-start(f32[128,128]{1,0:T(8,128)S(1)} %dynamic-slice_reduce_fusion.1), channel_id=1, source_target_pairs={{0,8},{4,12},{8,16},{12,20},{16,24},{20,28},{24,0},{28,4},{1,9},{5... | collective-permute-start | bytes 196616 | tf_op jit(solution)/shard_map/ppermute | solution.py:36
  313.4 18.5 %collective-permute-start.13 = (f32[128,128]{1,0:T(8,128)S(1)}, f32[128,128]{1,0:T(8,128)S(1)}, u32[]{:S(2)}, u32[]{:S(2)}) collective-permute-start(f32[128,128]{1,0:T(8,128)S(1)} %dynamic-slice_reduce_fusion.1), channel_id=1, source_target_pairs={{0,12},{4,16},{8,20},{12,24},{16,28},{20,0},{24,4},{28,8},{1,13},{... | collective-permute-start | bytes 196616 | tf_op jit(solution)/shard_map/ppermute | solution.py:36
  314.9 17.0 %collective-permute-start.12 = (f32[128,128]{1,0:T(8,128)S(1)}, f32[128,128]{1,0:T(8,128)S(1)}, u32[]{:S(2)}, u32[]{:S(2)}) collective-permute-start(f32[128,128]{1,0:T(8,128)S(1)} %dynamic-slice_reduce_fusion.1), channel_id=1, source_target_pairs={{0,16},{4,20},{8,24},{12,28},{16,0},{20,4},{24,8},{28,12},{1,17},{... | collective-permute-start | bytes 196616 | tf_op jit(solution)/shard_map/ppermute | solution.py:36
  317.2 4.3 %collective-permute-start.9 = (f32[128,128]{1,0:T(8,128)S(1)}, f32[128,128]{1,0:T(8,128)S(1)}, u32[]{:S(2)}, u32[]{:S(2)}) collective-permute-start(f32[128,128]{1,0:T(8,128)S(1)} %dynamic-slice_reduce_fusion.1), channel_id=1, source_target_pairs={{0,28},{4,0},{8,4},{12,8},{16,12},{20,16},{24,20},{28,24},{1,29},{... | collective-permute-start | bytes 196616 | tf_op jit(solution)/shard_map/ppermute | solution.py:36
  321.5 4.3 %collective-permute-start.10 = (f32[128,128]{1,0:T(8,128)S(1)}, f32[128,128]{1,0:T(8,128)S(1)}, u32[]{:S(2)}, u32[]{:S(2)}) collective-permute-start(f32[128,128]{1,0:T(8,128)S(1)} %dynamic-slice_reduce_fusion.1), channel_id=1, source_target_pairs={{0,24},{4,28},{8,0},{12,4},{16,8},{20,12},{24,16},{28,20},{1,25},{... | collective-permute-start | bytes 196616 | tf_op jit(solution)/shard_map/ppermute | solution.py:36
  325.8 6.1 %collective-permute-start.11 = (f32[128,128]{1,0:T(8,128)S(1)}, f32[128,128]{1,0:T(8,128)S(1)}, u32[]{:S(2)}, u32[]{:S(2)}) collective-permute-start(f32[128,128]{1,0:T(8,128)S(1)} %dynamic-slice_reduce_fusion.1), channel_id=1, source_target_pairs={{0,20},{4,24},{8,28},{12,0},{16,4},{20,8},{24,12},{28,16},{1,21},{... | collective-permute-start | bytes 196616 | tf_op jit(solution)/shard_map/ppermute | solution.py:36
  (2 other events, 1.3 us)
Sparse Core Ops, SparseCore 0:
  10.1 75.4 all-gather.1
  192.2 109.6 reduce-scatter.1

commit v2 on v0

--- a/solution.py
+++ b/solution.py
@@ -29,6 +29,23 @@
         send = lax.dynamic_index_in_dim(chunks, (me + k) % n, 0, keepdims=False)
         total = total + lax.ppermute(send, axis, shift_pairs(n, k))
     return total
+
+
+def pair_all_reduce(x, axis, n):
+    groups = n // 2
+    if n % 2 or groups & (groups - 1):
+        return lax.psum(x, axis)
+    inner = lax.axis_index(axis) % 2
+    halves = x.reshape(2, x.shape[0] // 2, *x.shape[1:])
+    keep = lax.dynamic_index_in_dim(halves, inner, 0, keepdims=False)
+    give = lax.dynamic_index_in_dim(halves, 1 - inner, 0, keepdims=False)
+    part = keep + lax.ppermute(give, axis, [(i, i ^ 1) for i in range(n)])
+    step = 2
+    while step < n:
+        part = part + lax.ppermute(part, axis, [(i, i ^ step) for i in range(n)])
+        step *= 2
+    other = lax.ppermute(part, axis, [(i, i ^ 1) for i in range(n)])
+    return jnp.roll(jnp.stack([part, other]), inner, axis=0).reshape(x.shape)
 
 
 def butterfly_sum(x, axes, n):
@@ -112,9 +129,12 @@
     )
     local_start = lax.axis_index("col") * local_rows
     local_weight = lax.dynamic_slice_in_dim(self_weight, local_start, local_rows, 0)
-    share_sum = ring_reduce_scatter(partial_value, "col", col_count)
-    projected = local_weight[:, None] * probe + share_sum
-    owner_y = ring_gather(projected, "col", col_count)
+    own_rows = lax.dynamic_slice_in_dim(partial_value, local_start, local_rows, 0)
+    partial_value = lax.dynamic_update_slice_in_dim(
+        partial_value, own_rows + local_weight[:, None] * probe, local_start, 0
+    )
+    owner_y = pair_all_reduce(partial_value, "col", col_count)
+    projected = lax.dynamic_slice_in_dim(owner_y, local_start, local_rows, 0)
     w_partial = slot_product(blocks, owner_y, block_row, block_col, counts, stripe_rows, True)
     w_share = lax.psum_scatter(w_partial, "row", scatter_dimension=0, tiled=True)
     sketch = local_weight[:, None] * projected + w_share

time: 355 us -> 330 us (0.930)
  waiting for transfers between devices: 240 us -> 207 us
  Pallas kernels: 37.6 us -> 67.2 us
  starting transfers between devices: 20.8 us -> 7.33 us
  local copies, waits for them, and re-layouts: 11.1 us -> 3.2 us
    pallas_call x2, Pallas kernels: 37.6 us -> 67.2 us  [slot_product(): pl.pallas_call(kernel, grid_spec=grid_spec, out_shape=jax.ShapeDtypeStruc...]
    reduce_scatter x1, waiting for transfers between devices: 105 us -> 86.9 us  [shards(): lax.psum_scatter(w_partial, 'row', scatter_dimension=0, tiled=True)]
    ppermute x6 -> x3, waiting for transfers between devices: 45.4 us -> 30.6 us  [the longest x1 25.2 us: pair_all_reduce(): part = part + lax.ppermute(part, axis, [(i, i ^ step) for i in range(n)])]
    ppermute x6 -> x3, starting transfers between devices: 13.6 us -> 0.21 us  [the longest x1 0.07 us: pair_all_reduce(): part = keep + lax.ppermute(give, axis, [(i, i ^ 1) for i in range(n)])]
    unnamed x20 -> x16, local copies, waits for them, and re-layouts: 6.61 us -> 2.3 us
  transfers between devices with their start and end apart: 13 -> 10, of which waited for: 12 -> 10; matrix products, arithmetic and copies ran while one was open for 1% -> 0% of each run, Pallas kernels for 0% -> 0%
where the time goes in v2:
time: 330 us
  waiting for transfers between devices  207 us (63%)
  Pallas kernels  67.2 us (20%)
  other arithmetic  26.6 us (8%)
  between operations  14.9 us (5%)
  starting transfers between devices  7.33 us (2%)
  matrix products  3.97 us (1%)
    reduce_scatter x1, waiting for transfers between devices, shards(): lax.psum_scatter(w_partial, 'row', scatter_dimension=0, tiled=True)  86.9 us
    all_gather x1, waiting for transfers between devices, shards(): stripe_probe = lax.all_gather(probe, 'row', axis=0, tiled=True)  76.3 us
    pallas_call x2, Pallas kernels, slot_product(): pl.pallas_call(kernel, grid_spec=grid_spec, out_shape=jax.ShapeDtypeStruc...  67.2 us
    ppermute x1, waiting for transfers between devices, pair_all_reduce(): part = part + lax.ppermute(part, axis, [(i, i ^ step) for i in range(n)])  25.2 us
    ppermute x5, waiting for transfers between devices, butterfly_sum(): x = x + lax.ppermute(x, axes, [(i, i ^ step) for i in range(n)])  12.5 us
    another operation x3, other arithmetic, shards(): lower = jnp.linalg.cholesky(gram)  12.4 us
    another operation x2, other arithmetic, shards(): lax.linalg.triangular_solve(lower, sketch, left_side=False, lower=True, t...  10.5 us
    ppermute x5, starting transfers between devices, butterfly_sum(): x = x + lax.ppermute(x, axes, [(i, i ^ step) for i in range(n)])  7.04 us
  transfers between devices with their start and end apart: 10, of which 10 were waited for; matrix products, arithmetic and copies ran while one was open for 0% of the time, Pallas kernels for 0%

profile of v2, /device:TPU:0, one launch (start us, length us, event | category | flops | bytes accessed | tf_op | source)
XLA Modules:
  0.0 330.3 jit_solution(11210428226905271050)
XLA Ops:
  8.6 0.7 dynamic_slice.21
  9.3 76.3 %all-gather.2.cloned.1.call-done.source_ref = f32[8192,128]{1,0:T(8,128)} async-done(((f32[1024,128]{1,0:T(8,128)}), f32[8192,128]{1,0:T(8,128)}) %all-gather.2.cloned.1.call-update) | async-done | bytes 4194320 | tf_op jit(solution)/shard_map/all_gather | solution.py:126
  87.0 29.7 %shard_map.77 = f32[4096,128]{1,0:T(8,128)S(1)} custom-call(s32[128]{0:T(128)S(1)} %copy-done, s32[128]{0:T(128)S(1)} %copy-done.2, s32[1]{0:T(128)S(6)} %copy.13.count_ref, f32[128,128,128]{2,1,0:T(8,128)} %block_ref.3, f32[8192,128]{1,0:T(8,128)} %all-gather.2.cloned.1.call-done.source_ref), custom_call_target="tpu_custom_call" | custom-call | tf_op jit(solution)/shard_map/pallas_call | solution.py:103
  117.1 2.8 collective-permute-done
  119.8 1.3 bitcast_add_fusion
  121.3 25.2 %collective-permute-done.1 = f32[2048,128]{1,0:T(8,128)S(1)} collective-permute-done((f32[2048,128]{1,0:T(8,128)S(1)}, f32[2048,128]{1,0:T(8,128)S(1)}, u32[]{:S(2)}, u32[]{:S(2)}) %collective-permute-start.1) | collective-permute-done | bytes 1048608 | tf_op jit(solution)/shard_map/ppermute | solution.py:45
  146.7 2.6 collective-permute-done.2
  149.3 1.0 copy-done.7
  150.3 2.0 fusion.2
  152.3 37.5 %shard_map.78 = f32[8192,128]{1,0:T(8,128)} custom-call(s32[128]{0:T(128)S(1)} %copy-done.1, s32[128]{0:T(128)S(1)} %copy-done.3, s32[1]{0:T(128)S(6)} %copy.13.count_ref, f32[128,128,128]{2,1,0:T(8,128)} %block_ref.3, f32[4096,128]{1,0:T(8,128)S(1)} %bitcast.17), custom_call_target="tpu_custom_call" | custom-call | tf_op jit(solution)/shard_map/pallas_call | solution.py:103
  189.9 86.9 %reduce-scatter.2.cloned.1.call-done = f32[1024,128]{1,0:T(8,128)} async-done(((f32[8192,128]{1,0:T(8,128)}), f32[1024,128]{1,0:T(8,128)}) %reduce-scatter.2.cloned.1.call-update) | async-done | bytes 524304 | tf_op jit(solution)/shard_map/reduce_scatter | solution.py:139
  276.8 2.6 fusion.3
  279.5 1.2 collective-permute-done.3
  280.7 1.5 collective-permute-start.4
  282.3 2.8 collective-permute-done.4
  285.1 1.5 collective-permute-start.5
  286.6 2.8 collective-permute-done.5
  289.4 1.8 collective-permute-start.6
  291.2 2.6 collective-permute-done.6
  293.8 2.2 collective-permute-start.7
  295.9 3.1 collective-permute-done.7
  299.1 11.7 %cholesky.16 = f32[128,128]{1,0:T(8,128)S(1)} custom-call(f32[128,128]{1,0:T(8,128)S(1)} %fusion.6), custom_call_target="Cholesky" | custom-call | tf_op jit(solution)/shard_map/jit(cholesky)/cholesky | solution.py:143
  312.2 9.8 %custom-call.6 = f32[1,128,128]{1,2,0:T(8,128)S(1)} custom-call(f32[1,128,128]{2,1,0:T(8,128)S(1)} %fusion.4), custom_call_target="InvertDiagBlocksLowerTriangular" | custom-call | tf_op jit(solution)/shard_map/triangular_solve | solution.py:144
  322.0 1.4 convolution_multiply_fusion
  (37 shorter events, 4.3 us)
Async XLA Ops:
  7.2 78.5 %all-gather.2.cloned.1.call-start = ((), (), s32[]{:S(2)}) async-start(), calls=%async_computation.1 | async-start | bytes 4718592 | tf_op jit(solution)/shard_map/all_gather | solution.py:126
  7.9 268.9 %reduce-scatter.2.cloned.1.call-start = ((), (), s32[]{:S(2)}) async-start(), calls=%async_computation.2 | async-start | bytes 4718592 | tf_op jit(solution)/shard_map/reduce_scatter | solution.py:139
  85.6 0.7 copy-start
  86.3 0.7 copy-start.2
  87.0 29.7 %copy-start.6 = (f32[1024,128]{1,0:T(8,128)S(1)}, f32[1024,128]{1,0:T(8,128)}, u32[]{:S(2)}) copy-start(f32[1024,128]{1,0:T(8,128)} %param.6) | copy-start | bytes 1572868
  117.0 2.9 collective-permute-start
  121.2 25.3 %collective-permute-start.1 = (f32[2048,128]{1,0:T(8,128)S(1)}, f32[2048,128]{1,0:T(8,128)S(1)}, u32[]{:S(2)}, u32[]{:S(2)}) collective-permute-start(f32[2048,128]{1,0:T(8,128)S(1)} %bitcast_add_fusion), channel_id=1, source_target_pairs={{0,2},{1,3},{2,0},{3,1},{4,6},{5,7},{6,4},{7,5},{8,10},{9,11},{10,... | collective-permute-start | bytes 3145736 | tf_op jit(solution)/shard_map/ppermute | solution.py:45
  146.6 2.7 collective-permute-start.2
  149.3 1.0 copy-start.7
  150.3 2.0 copy-start.1
  150.3 2.0 copy-start.3
  189.9 133.5 %copy-start.4 = (f32[1024,128]{1,0:T(8,128)}, f32[1024,128]{1,0:T(8,128)S(1)}, u32[]{:S(2)}) copy-start(f32[1024,128]{1,0:T(8,128)S(1)} %constant_dynamic-slice_fusion) | copy-start | bytes 1572868
  276.8 45.2 %copy-start.5 = (f32[1024,128]{1,0:T(8,128)S(1)}, f32[1024,128]{1,0:T(8,128)}, u32[]{:S(2)}) copy-start(f32[1024,128]{1,0:T(8,128)} %reduce-scatter.2.cloned.1.call-done) | copy-start | bytes 1572868
  279.4 1.3 collective-permute-start.3
  280.7 4.3 %collective-permute-start.4 = (f32[128,128]{0,1:T(8,128)S(1)}, f32[128,128]{0,1:T(8,128)S(1)}, u32[]{:S(2)}, u32[]{:S(2)}) collective-permute-start(f32[128,128]{0,1:T(8,128)S(1)} %add.78), channel_id=1, source_target_pairs={{0,2},{1,3},{2,0},{3,1},{4,6},{5,7},{6,4},{7,5},{8,10},{9,11},{10,... | collective-permute-start | bytes 196616 | tf_op jit(solution)/shard_map/ppermute | solution.py:56
  285.1 4.3 %collective-permute-start.5 = (f32[128,128]{0,1:T(8,128)S(1)}, f32[128,128]{0,1:T(8,128)S(1)}, u32[]{:S(2)}, u32[]{:S(2)}) collective-permute-start(f32[128,128]{0,1:T(8,128)S(1)} %add.79), channel_id=1, source_target_pairs={{0,4},{1,5},{2,6},{3,7},{4,0},{5,1},{6,2},{7,3},{8,12},{9,13},{10,... | collective-permute-start | bytes 196616 | tf_op jit(solution)/shard_map/ppermute | solution.py:56
  289.4 4.3 %collective-permute-start.6 = (f32[128,128]{0,1:T(8,128)S(1)}, f32[128,128]{0,1:T(8,128)S(1)}, u32[]{:S(2)}, u32[]{:S(2)}) collective-permute-start(f32[128,128]{0,1:T(8,128)S(1)} %add.80), channel_id=1, source_target_pairs={{0,8},{1,9},{2,10},{3,11},{4,12},{5,13},{6,14},{7,15},{8,0},{9,1},... | collective-permute-start | bytes 196616 | tf_op jit(solution)/shard_map/ppermute | solution.py:56
  293.8 5.2 %collective-permute-start.7 = (f32[128,128]{0,1:T(8,128)S(1)}, f32[128,128]{0,1:T(8,128)S(1)}, u32[]{:S(2)}, u32[]{:S(2)}) collective-permute-start(f32[128,128]{0,1:T(8,128)S(1)} %add.81), channel_id=1, source_target_pairs={{0,16},{1,17},{2,18},{3,19},{4,20},{5,21},{6,22},{7,23},{8,24},{9,... | collective-permute-start | bytes 196616 | tf_op jit(solution)/shard_map/ppermute | solution.py:56
Sparse Core Ops, SparseCore 0:
  10.1 75.4 all-gather.1
  189.9 86.8 reduce-scatter.1

commit v3 on v2

--- a/solution.py
+++ b/solution.py
@@ -9,6 +9,7 @@
 
 PRECISE = lax.Precision.HIGHEST
 INTERPRET = False
+KERNEL_PRECISION = lax.Precision.HIGH
 
 
 def shift_pairs(n, k):
@@ -61,7 +62,7 @@
 def slot_product(blocks, source, block_row, block_col, counts, out_rows, transpose):
     slot_count, block_size = blocks.shape[0], blocks.shape[1]
     width = source.shape[1]
-    group = 8 if slot_count % 8 == 0 else 1
+    group = 32 if slot_count % 32 == 0 else 1
 
     def kernel(row_ref, col_ref, count_ref, block_ref, source_ref, out_ref):
         step = pl.program_id(0)
@@ -82,7 +83,7 @@
                 if transpose:
                     block = block.T
                 product = jnp.dot(
-                    block, piece, precision=PRECISE, preferred_element_type=jnp.float32
+                    block, piece, precision=KERNEL_PRECISION, preferred_element_type=jnp.float32
                 )
                 at = pl.ds(pl.multiple_of(write * block_size, block_size), block_size)
                 out_ref[at, :] = out_ref[at, :] + product

time: 330 us -> 322 us (0.976)
  Pallas kernels: 67.2 us -> 59.1 us
    pallas_call x2, Pallas kernels: 67.2 us -> 59.1 us  [slot_product(): pl.pallas_call(kernel, grid_spec=grid_spec, out_shape=jax.ShapeDtypeStruc...]
where the time goes in v3:
time: 322 us
  waiting for transfers between devices  207 us (64%)
  Pallas kernels  59.1 us (18%)
  other arithmetic  26.6 us (8%)
  between operations  14.9 us (5%)
  starting transfers between devices  7.34 us (2%)
  matrix products  3.98 us (1%)
    reduce_scatter x1, waiting for transfers between devices, shards(): lax.psum_scatter(w_partial, 'row', scatter_dimension=0, tiled=True)  87 us
    all_gather x1, waiting for transfers between devices, shards(): stripe_probe = lax.all_gather(probe, 'row', axis=0, tiled=True)  76.3 us
    pallas_call x2, Pallas kernels, slot_product(): pl.pallas_call(kernel, grid_spec=grid_spec, out_shape=jax.ShapeDtypeStruc...  59.1 us
    ppermute x1, waiting for transfers between devices, pair_all_reduce(): part = part + lax.ppermute(part, axis, [(i, i ^ step) for i in range(n)])  25.2 us
    ppermute x5, waiting for transfers between devices, butterfly_sum(): x = x + lax.ppermute(x, axes, [(i, i ^ step) for i in range(n)])  12.5 us
    another operation x3, other arithmetic, shards(): lower = jnp.linalg.cholesky(gram)  12.4 us
    another operation x2, other arithmetic, shards(): lax.linalg.triangular_solve(lower, sketch, left_side=False, lower=True, t...  10.5 us
    ppermute x5, starting transfers between devices, butterfly_sum(): x = x + lax.ppermute(x, axes, [(i, i ^ step) for i in range(n)])  7.05 us
  transfers between devices with their start and end apart: 10, of which 10 were waited for; matrix products, arithmetic and copies ran while one was open for 0% of the time, Pallas kernels for 0%

profile of v3, /device:TPU:0, one launch (start us, length us, event | category | flops | bytes accessed | tf_op | source)
XLA Modules:
  0.0 322.2 jit_solution(13913274975855689454)
XLA Ops:
  8.6 0.7 dynamic_slice.21
  9.3 76.3 %all-gather.2.cloned.1.call-done.source_ref = f32[8192,128]{1,0:T(8,128)} async-done(((f32[1024,128]{1,0:T(8,128)}), f32[8192,128]{1,0:T(8,128)}) %all-gather.2.cloned.1.call-update) | async-done | bytes 4194320 | tf_op jit(solution)/shard_map/all_gather | solution.py:127
  87.0 25.6 %shard_map.77 = f32[4096,128]{1,0:T(8,128)S(1)} custom-call(s32[128]{0:T(128)S(1)} %copy-done, s32[128]{0:T(128)S(1)} %copy-done.2, s32[1]{0:T(128)S(6)} %copy.13.count_ref, f32[128,128,128]{2,1,0:T(8,128)} %block_ref.3, f32[8192,128]{1,0:T(8,128)} %all-gather.2.cloned.1.call-done.source_ref), custom_call_target="tpu_custom_call" | custom-call | tf_op jit(solution)/shard_map/pallas_call | solution.py:104
  113.0 2.8 collective-permute-done
  115.7 1.3 bitcast_add_fusion
  117.2 25.2 %collective-permute-done.1 = f32[2048,128]{1,0:T(8,128)S(1)} collective-permute-done((f32[2048,128]{1,0:T(8,128)S(1)}, f32[2048,128]{1,0:T(8,128)S(1)}, u32[]{:S(2)}, u32[]{:S(2)}) %collective-permute-start.1) | collective-permute-done | bytes 1048608 | tf_op jit(solution)/shard_map/ppermute | solution.py:46
  142.6 2.6 collective-permute-done.2
  145.2 1.0 copy-done.7
  146.2 2.0 fusion.2
  148.2 33.5 %shard_map.78 = f32[8192,128]{1,0:T(8,128)} custom-call(s32[128]{0:T(128)S(1)} %copy-done.1, s32[128]{0:T(128)S(1)} %copy-done.3, s32[1]{0:T(128)S(6)} %copy.13.count_ref, f32[128,128,128]{2,1,0:T(8,128)} %block_ref.3, f32[4096,128]{1,0:T(8,128)S(1)} %bitcast.17), custom_call_target="tpu_custom_call" | custom-call | tf_op jit(solution)/shard_map/pallas_call | solution.py:104
  181.8 87.0 %reduce-scatter.2.cloned.1.call-done = f32[1024,128]{1,0:T(8,128)} async-done(((f32[8192,128]{1,0:T(8,128)}), f32[1024,128]{1,0:T(8,128)}) %reduce-scatter.2.cloned.1.call-update) | async-done | bytes 524304 | tf_op jit(solution)/shard_map/reduce_scatter | solution.py:140
  268.7 2.6 fusion.3
  271.4 1.2 collective-permute-done.3
  272.6 1.5 collective-permute-start.4
  274.2 2.8 collective-permute-done.4
  277.0 1.5 collective-permute-start.5
  278.5 2.8 collective-permute-done.5
  281.3 1.8 collective-permute-start.6
  283.1 2.6 collective-permute-done.6
  285.7 2.2 collective-permute-start.7
  287.8 3.1 collective-permute-done.7
  291.0 11.7 %cholesky.16 = f32[128,128]{1,0:T(8,128)S(1)} custom-call(f32[128,128]{1,0:T(8,128)S(1)} %fusion.6), custom_call_target="Cholesky" | custom-call | tf_op jit(solution)/shard_map/jit(cholesky)/cholesky | solution.py:144
  304.1 9.8 %custom-call.6 = f32[1,128,128]{1,2,0:T(8,128)S(1)} custom-call(f32[1,128,128]{2,1,0:T(8,128)S(1)} %fusion.4), custom_call_target="InvertDiagBlocksLowerTriangular" | custom-call | tf_op jit(solution)/shard_map/triangular_solve | solution.py:145
  313.9 1.4 convolution_multiply_fusion
  (37 shorter events, 4.3 us)
Async XLA Ops:
  7.2 78.5 %all-gather.2.cloned.1.call-start = ((), (), s32[]{:S(2)}) async-start(), calls=%async_computation.1 | async-start | bytes 4718592 | tf_op jit(solution)/shard_map/all_gather | solution.py:127
  7.9 260.8 %reduce-scatter.2.cloned.1.call-start = ((), (), s32[]{:S(2)}) async-start(), calls=%async_computation.2 | async-start | bytes 4718592 | tf_op jit(solution)/shard_map/reduce_scatter | solution.py:140
  85.6 0.7 copy-start
  86.3 0.7 copy-start.2
  87.0 25.6 %copy-start.6 = (f32[1024,128]{1,0:T(8,128)S(1)}, f32[1024,128]{1,0:T(8,128)}, u32[]{:S(2)}) copy-start(f32[1024,128]{1,0:T(8,128)} %param.6) | copy-start | bytes 1572868
  112.9 2.9 collective-permute-start
  117.1 25.3 %collective-permute-start.1 = (f32[2048,128]{1,0:T(8,128)S(1)}, f32[2048,128]{1,0:T(8,128)S(1)}, u32[]{:S(2)}, u32[]{:S(2)}) collective-permute-start(f32[2048,128]{1,0:T(8,128)S(1)} %bitcast_add_fusion), channel_id=1, source_target_pairs={{0,2},{1,3},{2,0},{3,1},{4,6},{5,7},{6,4},{7,5},{8,10},{9,11},{10,... | collective-permute-start | bytes 3145736 | tf_op jit(solution)/shard_map/ppermute | solution.py:46
  142.5 2.7 collective-permute-start.2
  145.2 1.0 copy-start.7
  146.1 2.0 copy-start.1
  146.2 2.0 copy-start.3
  181.8 133.6 %copy-start.4 = (f32[1024,128]{1,0:T(8,128)}, f32[1024,128]{1,0:T(8,128)S(1)}, u32[]{:S(2)}) copy-start(f32[1024,128]{1,0:T(8,128)S(1)} %constant_dynamic-slice_fusion) | copy-start | bytes 1572868
  268.7 45.2 %copy-start.5 = (f32[1024,128]{1,0:T(8,128)S(1)}, f32[1024,128]{1,0:T(8,128)}, u32[]{:S(2)}) copy-start(f32[1024,128]{1,0:T(8,128)} %reduce-scatter.2.cloned.1.call-done) | copy-start | bytes 1572868
  271.3 1.3 collective-permute-start.3
  272.6 4.3 %collective-permute-start.4 = (f32[128,128]{0,1:T(8,128)S(1)}, f32[128,128]{0,1:T(8,128)S(1)}, u32[]{:S(2)}, u32[]{:S(2)}) collective-permute-start(f32[128,128]{0,1:T(8,128)S(1)} %add.78), channel_id=1, source_target_pairs={{0,2},{1,3},{2,0},{3,1},{4,6},{5,7},{6,4},{7,5},{8,10},{9,11},{10,... | collective-permute-start | bytes 196616 | tf_op jit(solution)/shard_map/ppermute | solution.py:57
  277.0 4.3 %collective-permute-start.5 = (f32[128,128]{0,1:T(8,128)S(1)}, f32[128,128]{0,1:T(8,128)S(1)}, u32[]{:S(2)}, u32[]{:S(2)}) collective-permute-start(f32[128,128]{0,1:T(8,128)S(1)} %add.79), channel_id=1, source_target_pairs={{0,4},{1,5},{2,6},{3,7},{4,0},{5,1},{6,2},{7,3},{8,12},{9,13},{10,... | collective-permute-start | bytes 196616 | tf_op jit(solution)/shard_map/ppermute | solution.py:57
  281.3 4.3 %collective-permute-start.6 = (f32[128,128]{0,1:T(8,128)S(1)}, f32[128,128]{0,1:T(8,128)S(1)}, u32[]{:S(2)}, u32[]{:S(2)}) collective-permute-start(f32[128,128]{0,1:T(8,128)S(1)} %add.80), channel_id=1, source_target_pairs={{0,8},{1,9},{2,10},{3,11},{4,12},{5,13},{6,14},{7,15},{8,0},{9,1},... | collective-permute-start | bytes 196616 | tf_op jit(solution)/shard_map/ppermute | solution.py:57
  285.7 5.2 %collective-permute-start.7 = (f32[128,128]{0,1:T(8,128)S(1)}, f32[128,128]{0,1:T(8,128)S(1)}, u32[]{:S(2)}, u32[]{:S(2)}) collective-permute-start(f32[128,128]{0,1:T(8,128)S(1)} %add.81), channel_id=1, source_target_pairs={{0,16},{1,17},{2,18},{3,19},{4,20},{5,21},{6,22},{7,23},{8,24},{9,... | collective-permute-start | bytes 196616 | tf_op jit(solution)/shard_map/ppermute | solution.py:57
Sparse Core Ops, SparseCore 0:
  10.1 75.4 all-gather.1
  181.8 86.8 reduce-scatter.1

commit v4 on v3

--- a/solution.py
+++ b/solution.py
@@ -75,19 +75,18 @@
             slot = step * group + s
             read = row_ref[slot] if transpose else col_ref[slot]
             write = col_ref[slot] if transpose else row_ref[slot]
-
-            @pl.when(slot < count_ref[0])
-            def _():
-                piece = source_ref[pl.ds(pl.multiple_of(read * block_size, block_size), block_size), :]
-                block = block_ref[s]
-                if transpose:
-                    block = block.T
-                product = jnp.dot(
-                    block, piece, precision=KERNEL_PRECISION, preferred_element_type=jnp.float32
-                )
-                at = pl.ds(pl.multiple_of(write * block_size, block_size), block_size)
-                out_ref[at, :] = out_ref[at, :] + product
-
+            read = jnp.clip(read, 0, source_ref.shape[0] // block_size - 1)
+            write = jnp.clip(write, 0, out_ref.shape[0] // block_size - 1)
+            live = (slot < count_ref[0]).astype(jnp.float32)
+            piece = source_ref[pl.ds(pl.multiple_of(read * block_size, block_size), block_size), :]
+            block = block_ref[s]
+            if transpose:
+                block = block.T
+            product = jnp.dot(
+                block, piece, precision=KERNEL_PRECISION, preferred_element_type=jnp.float32
+            )
+            at = pl.ds(pl.multiple_of(write * block_size, block_size), block_size)
+            out_ref[at, :] = out_ref[at, :] + product * live
             return carry
 
         lax.fori_loop(0, group, body, 0, unroll=True)

time: 322 us -> 282 us (0.88)
  Pallas kernels: 59.1 us -> 18.1 us
    pallas_call x2, Pallas kernels: 59.1 us -> 18.1 us  [slot_product(): pl.pallas_call(kernel, grid_spec=grid_spec, out_shape=jax.ShapeDtypeStruc...]
where the time goes in v4:
time: 282 us; the launch traced here: 281 us
  waiting for transfers between devices  205 us (73%)
  other arithmetic  26.6 us (9%)
  Pallas kernels  18.1 us (6%)
  between operations  14.9 us (5%)
  starting transfers between devices  8.91 us (3%)
  matrix products  3.98 us (1%)
  local copies, waits for them, and re-layouts  3.2 us (1%)
    reduce_scatter x1, waiting for transfers between devices, shards(): lax.psum_scatter(w_partial, 'row', scatter_dimension=0, tiled=True)  87 us
    all_gather x1, waiting for transfers between devices, shards(): stripe_probe = lax.all_gather(probe, 'row', axis=0, tiled=True)  76.3 us
    ppermute x1, waiting for transfers between devices, pair_all_reduce(): part = part + lax.ppermute(part, axis, [(i, i ^ step) for i in range(n)])  23.7 us
    pallas_call x2, Pallas kernels, slot_product(): pl.pallas_call(kernel, grid_spec=grid_spec, out_shape=jax.ShapeDtypeStruc...  18.1 us
    another operation x3, other arithmetic, shards(): lower = jnp.linalg.cholesky(gram)  12.4 us
    ppermute x5, waiting for transfers between devices, butterfly_sum(): x = x + lax.ppermute(x, axes, [(i, i ^ step) for i in range(n)])  12.4 us
    another operation x2, other arithmetic, shards(): lax.linalg.triangular_solve(lower, sketch, left_side=False, lower=True, t...  10.5 us
    ppermute x5, starting transfers between devices, butterfly_sum(): x = x + lax.ppermute(x, axes, [(i, i ^ step) for i in range(n)])  7.16 us
  transfers between devices with their start and end apart: 10, of which 10 were waited for; matrix products, arithmetic and copies ran while one was open for 0% of the time, Pallas kernels for 0%

profile of v4, /device:TPU:0, one launch (start us, length us, event | category | flops | bytes accessed | tf_op | source)
XLA Modules:
  0.0 281.2 jit_solution(2345021602027749164)
XLA Ops:
  9.3 76.3 %all-gather.2.cloned.1.call-done.source_ref = f32[8192,128]{1,0:T(8,128)} async-done(((f32[1024,128]{1,0:T(8,128)}), f32[8192,128]{1,0:T(8,128)}) %all-gather.2.cloned.1.call-update) | async-done | bytes 4194320 | tf_op jit(solution)/shard_map/all_gather | solution.py:126
  87.0 8.4 %shard_map.77 = f32[4096,128]{1,0:T(8,128)S(1)} custom-call(s32[128]{0:T(128)S(1)} %copy-done, s32[128]{0:T(128)S(1)} %copy-done.2, s32[1]{0:T(128)S(6)} %copy.13.count_ref, f32[128,128,128]{2,1,0:T(8,128)} %block_ref.3, f32[8192,128]{1,0:T(8,128)} %all-gather.2.cloned.1.call-done.source_ref), custom_call_target="tpu_custom_call" | custom-call | tf_op jit(solution)/shard_map/pallas_call | solution.py:103
  95.8 2.8 collective-permute-done
  98.6 1.3 bitcast_add_fusion
  99.9 1.5 collective-permute-start.1
  101.4 23.7 %collective-permute-done.1 = f32[2048,128]{1,0:T(8,128)S(1)} collective-permute-done((f32[2048,128]{1,0:T(8,128)S(1)}, f32[2048,128]{1,0:T(8,128)S(1)}, u32[]{:S(2)}, u32[]{:S(2)}) %collective-permute-start.1) | collective-permute-done | bytes 1048608 | tf_op jit(solution)/shard_map/ppermute | solution.py:46
  125.4 2.6 collective-permute-done.2
  128.0 1.0 copy-done.7
  129.0 2.0 fusion.2
  131.0 9.7 %shard_map.78 = f32[8192,128]{1,0:T(8,128)} custom-call(s32[128]{0:T(128)S(1)} %copy-done.1, s32[128]{0:T(128)S(1)} %copy-done.3, s32[1]{0:T(128)S(6)} %copy.13.count_ref, f32[128,128,128]{2,1,0:T(8,128)} %block_ref.3, f32[4096,128]{1,0:T(8,128)S(1)} %bitcast.17), custom_call_target="tpu_custom_call" | custom-call | tf_op jit(solution)/shard_map/pallas_call | solution.py:103
  140.8 87.0 %reduce-scatter.2.cloned.1.call-done = f32[1024,128]{1,0:T(8,128)} async-done(((f32[8192,128]{1,0:T(8,128)}), f32[1024,128]{1,0:T(8,128)}) %reduce-scatter.2.cloned.1.call-update) | async-done | bytes 524304 | tf_op jit(solution)/shard_map/reduce_scatter | solution.py:139
  227.8 2.6 fusion.3
  230.4 1.2 collective-permute-done.3
  231.7 1.6 collective-permute-start.4
  233.2 2.8 collective-permute-done.4
  236.0 1.5 collective-permute-start.5
  237.6 2.8 collective-permute-done.5
  240.4 1.8 collective-permute-start.6
  242.1 2.6 collective-permute-done.6
  244.7 2.2 collective-permute-start.7
  246.9 3.0 %collective-permute-done.7 = f32[128,128]{0,1:T(8,128)S(1)} collective-permute-done((f32[128,128]{0,1:T(8,128)S(1)}, f32[128,128]{0,1:T(8,128)S(1)}, u32[]{:S(2)}, u32[]{:S(2)}) %collective-permute-start.7) | collective-permute-done | bytes 65568 | tf_op jit(solution)/shard_map/ppermute | solution.py:57
  250.1 11.7 %cholesky.16 = f32[128,128]{1,0:T(8,128)S(1)} custom-call(f32[128,128]{1,0:T(8,128)S(1)} %fusion.6), custom_call_target="Cholesky" | custom-call | tf_op jit(solution)/shard_map/jit(cholesky)/cholesky | solution.py:143
  263.1 9.8 %custom-call.6 = f32[1,128,128]{1,2,0:T(8,128)S(1)} custom-call(f32[1,128,128]{2,1,0:T(8,128)S(1)} %fusion.4), custom_call_target="InvertDiagBlocksLowerTriangular" | custom-call | tf_op jit(solution)/shard_map/triangular_solve | solution.py:144
  272.9 1.4 convolution_multiply_fusion
  (37 shorter events, 5.0 us)
Async XLA Ops:
  7.2 78.5 %all-gather.2.cloned.1.call-start = ((), (), s32[]{:S(2)}) async-start(), calls=%async_computation.1 | async-start | bytes 4718592 | tf_op jit(solution)/shard_map/all_gather | solution.py:126
  7.9 219.9 %reduce-scatter.2.cloned.1.call-start = ((), (), s32[]{:S(2)}) async-start(), calls=%async_computation.2 | async-start | bytes 4718592 | tf_op jit(solution)/shard_map/reduce_scatter | solution.py:139
  85.6 0.7 copy-start
  86.3 0.7 copy-start.2
  87.0 8.4 %copy-start.6 = (f32[1024,128]{1,0:T(8,128)S(1)}, f32[1024,128]{1,0:T(8,128)}, u32[]{:S(2)}) copy-start(f32[1024,128]{1,0:T(8,128)} %param.6) | copy-start | bytes 1572868
  95.7 2.9 %collective-permute-start = (f32[2048,128]{1,0:T(8,128)S(1)}, f32[2048,128]{1,0:T(8,128)}, u32[]{:S(2)}, u32[]{:S(2)}) collective-permute-start(f32[2048,128]{1,0:T(8,128)S(1)} %dynamic-slice_bitcast_fusion), channel_id=1, source_target_pairs={{0,1},{1,0},{2,3},{3,2},{4,5},{5,4},{6,7},{7,6},{8,9},{9,8},{10,11... | collective-permute-start | bytes 3145736 | tf_op jit(solution)/shard_map/ppermute | solution.py:43
  99.9 25.3 %collective-permute-start.1 = (f32[2048,128]{1,0:T(8,128)S(1)}, f32[2048,128]{1,0:T(8,128)S(1)}, u32[]{:S(2)}, u32[]{:S(2)}) collective-permute-start(f32[2048,128]{1,0:T(8,128)S(1)} %bitcast_add_fusion), channel_id=1, source_target_pairs={{0,2},{1,3},{2,0},{3,1},{4,6},{5,7},{6,4},{7,5},{8,10},{9,11},{10,... | collective-permute-start | bytes 3145736 | tf_op jit(solution)/shard_map/ppermute | solution.py:46
  125.3 2.7 collective-permute-start.2
  128.0 1.0 copy-start.7
  129.0 2.0 copy-start.1
  129.0 2.0 copy-start.3
  140.8 133.6 %copy-start.4 = (f32[1024,128]{1,0:T(8,128)}, f32[1024,128]{1,0:T(8,128)S(1)}, u32[]{:S(2)}) copy-start(f32[1024,128]{1,0:T(8,128)S(1)} %constant_dynamic-slice_fusion) | copy-start | bytes 1572868
  227.8 45.2 %copy-start.5 = (f32[1024,128]{1,0:T(8,128)S(1)}, f32[1024,128]{1,0:T(8,128)}, u32[]{:S(2)}) copy-start(f32[1024,128]{1,0:T(8,128)} %reduce-scatter.2.cloned.1.call-done) | copy-start | bytes 1572868
  230.3 1.3 collective-permute-start.3
  231.7 4.3 %collective-permute-start.4 = (f32[128,128]{0,1:T(8,128)S(1)}, f32[128,128]{0,1:T(8,128)S(1)}, u32[]{:S(2)}, u32[]{:S(2)}) collective-permute-start(f32[128,128]{0,1:T(8,128)S(1)} %add.78), channel_id=1, source_target_pairs={{0,2},{1,3},{2,0},{3,1},{4,6},{5,7},{6,4},{7,5},{8,10},{9,11},{10,... | collective-permute-start | bytes 196616 | tf_op jit(solution)/shard_map/ppermute | solution.py:57
  236.0 4.3 %collective-permute-start.5 = (f32[128,128]{0,1:T(8,128)S(1)}, f32[128,128]{0,1:T(8,128)S(1)}, u32[]{:S(2)}, u32[]{:S(2)}) collective-permute-start(f32[128,128]{0,1:T(8,128)S(1)} %add.79), channel_id=1, source_target_pairs={{0,4},{1,5},{2,6},{3,7},{4,0},{5,1},{6,2},{7,3},{8,12},{9,13},{10,... | collective-permute-start | bytes 196616 | tf_op jit(solution)/shard_map/ppermute | solution.py:57
  240.4 4.3 %collective-permute-start.6 = (f32[128,128]{0,1:T(8,128)S(1)}, f32[128,128]{0,1:T(8,128)S(1)}, u32[]{:S(2)}, u32[]{:S(2)}) collective-permute-start(f32[128,128]{0,1:T(8,128)S(1)} %add.80), channel_id=1, source_target_pairs={{0,8},{1,9},{2,10},{3,11},{4,12},{5,13},{6,14},{7,15},{8,0},{9,1},... | collective-permute-start | bytes 196616 | tf_op jit(solution)/shard_map/ppermute | solution.py:57
  244.7 5.2 %collective-permute-start.7 = (f32[128,128]{0,1:T(8,128)S(1)}, f32[128,128]{0,1:T(8,128)S(1)}, u32[]{:S(2)}, u32[]{:S(2)}) collective-permute-start(f32[128,128]{0,1:T(8,128)S(1)} %add.81), channel_id=1, source_target_pairs={{0,16},{1,17},{2,18},{3,19},{4,20},{5,21},{6,22},{7,23},{8,24},{9,... | collective-permute-start | bytes 196616 | tf_op jit(solution)/shard_map/ppermute | solution.py:57
Sparse Core Ops, SparseCore 0:
  10.1 75.4 all-gather.1
  140.9 86.8 reduce-scatter.1

commit v5 on v4

--- a/solution.py
+++ b/solution.py
@@ -43,7 +43,9 @@
     part = keep + lax.ppermute(give, axis, [(i, i ^ 1) for i in range(n)])
     step = 2
     while step < n:
-        part = part + lax.ppermute(part, axis, [(i, i ^ step) for i in range(n)])
+        pairs = [(i, i ^ step) for i in range(n)]
+        pieces = jnp.split(part, 2) if part.shape[0] % 2 == 0 else [part]
+        part = jnp.concatenate([p + lax.ppermute(p, axis, pairs) for p in pieces])
         step *= 2
     other = lax.ppermute(part, axis, [(i, i ^ 1) for i in range(n)])
     return jnp.roll(jnp.stack([part, other]), inner, axis=0).reshape(x.shape)
@@ -141,9 +143,10 @@
     gram_part = jnp.dot(sketch.T, sketch, precision=PRECISE, preferred_element_type=jnp.float32)
     gram = butterfly_sum(gram_part, ("row", "col"), row_count * col_count)
     lower = jnp.linalg.cholesky(gram)
-    solved = lax.linalg.triangular_solve(
-        lower, sketch, left_side=False, lower=True, transpose_a=True
+    lower_inverse = lax.linalg.triangular_solve(
+        lower, jnp.eye(lower.shape[0], dtype=lower.dtype), left_side=True, lower=True
     )
+    solved = jnp.dot(sketch, lower_inverse.T, precision=PRECISE)
     basis = solved * math.sqrt(answers)
     return (projected, basis)
 

time: 282 us -> 282 us (level)
    ppermute x1 -> x2, waiting for transfers between devices: 23.7 us -> 23.2 us  [pair_all_reduce(): part = jnp.concatenate([p + lax.ppermute(p, axis, pairs) for p in pieces])]
  transfers between devices with their start and end apart: 10 -> 11, of which waited for: 10 -> 11; matrix products, arithmetic and copies ran while one was open for 0% -> 0% of each run, Pallas kernels for 0% -> 0%
where the time goes in v5:
time: 282 us
  waiting for transfers between devices  205 us (73%)
  other arithmetic  26.8 us (10%)
  Pallas kernels  18.2 us (6%)
  between operations  14.9 us (5%)
  starting transfers between devices  9.46 us (3%)
  matrix products  4.22 us (1%)
  local copies, waits for them, and re-layouts  3.29 us (1%)
    reduce_scatter x1, waiting for transfers between devices, shards(): lax.psum_scatter(w_partial, 'row', scatter_dimension=0, tiled=True)  86.9 us
    all_gather x1, waiting for transfers between devices, shards(): stripe_probe = lax.all_gather(probe, 'row', axis=0, tiled=True)  76.3 us
    ppermute x2, waiting for transfers between devices, pair_all_reduce(): part = jnp.concatenate([p + lax.ppermute(p, axis, pairs) for p in pieces])  23.2 us
    pallas_call x2, Pallas kernels, slot_product(): pl.pallas_call(kernel, grid_spec=grid_spec, out_shape=jax.ShapeDtypeStruc...  18.2 us
    another operation x3, other arithmetic, shards(): lower = jnp.linalg.cholesky(gram)  12.4 us
    ppermute x5, waiting for transfers between devices, butterfly_sum(): x = x + lax.ppermute(x, axes, [(i, i ^ step) for i in range(n)])  12.4 us
    another operation x2, other arithmetic, shards(): lax.linalg.triangular_solve(lower, jnp.eye(lower.shape[0], dtype=lower.dt...  10.5 us
    ppermute x5, starting transfers between devices, butterfly_sum(): x = x + lax.ppermute(x, axes, [(i, i ^ step) for i in range(n)])  7.15 us
  transfers between devices with their start and end apart: 11, of which 11 were waited for; matrix products, arithmetic and copies ran while one was open for 0% of the time, Pallas kernels for 0%

profile of v5, /device:TPU:0, one launch (start us, length us, event | category | flops | bytes accessed | tf_op | source)
XLA Modules:
  0.0 281.7 jit_solution(6230342722164150403)
XLA Ops:
  9.3 76.3 %all-gather.2.cloned.1.call-done.source_ref = f32[8192,128]{1,0:T(8,128)} async-done(((f32[1024,128]{1,0:T(8,128)}), f32[8192,128]{1,0:T(8,128)}) %all-gather.2.cloned.1.call-update) | async-done | bytes 4194320 | tf_op jit(solution)/shard_map/all_gather | solution.py:128
  87.0 8.4 %shard_map.77 = f32[4096,128]{1,0:T(8,128)S(1)} custom-call(s32[128]{0:T(128)S(1)} %copy-done, s32[128]{0:T(128)S(1)} %copy-done.2, s32[1]{0:T(128)S(6)} %copy.13.count_ref, f32[128,128,128]{2,1,0:T(8,128)} %block_ref.3, f32[8192,128]{1,0:T(8,128)} %all-gather.2.cloned.1.call-done.source_ref), custom_call_target="tpu_custom_call" | custom-call | tf_op jit(solution)/shard_map/pallas_call | solution.py:105
  95.8 2.8 collective-permute-done
  98.6 1.3 bitcast_add_fusion
  100.0 1.5 collective-permute-start.1
  102.1 12.8 %collective-permute-done.1 = f32[1024,128]{1,0:T(8,128)S(1)} collective-permute-done((f32[1024,128]{1,0:T(8,128)S(1)}, f32[1024,128]{1,0:T(8,128)S(1)}, u32[]{:S(2)}, u32[]{:S(2)}) %collective-permute-start.1) | collective-permute-done | bytes 524320 | tf_op jit(solution)/shard_map/ppermute | solution.py:48
  114.8 10.4 %collective-permute-done.2 = f32[1024,128]{1,0:T(8,128)S(1)} collective-permute-done((f32[1024,128]{1,0:T(8,128)S(1)}, f32[1024,128]{1,0:T(8,128)S(1)}, u32[]{:S(2)}, u32[]{:S(2)}) %collective-permute-start.2) | collective-permute-done | bytes 524320 | tf_op jit(solution)/shard_map/ppermute | solution.py:48
  125.6 2.6 collective-permute-done.3
  129.2 2.0 fusion.2
  131.3 9.7 %shard_map.78 = f32[8192,128]{1,0:T(8,128)} custom-call(s32[128]{0:T(128)S(1)} %copy-done.1, s32[128]{0:T(128)S(1)} %copy-done.3, s32[1]{0:T(128)S(6)} %copy.13.count_ref, f32[128,128,128]{2,1,0:T(8,128)} %block_ref.3, f32[4096,128]{1,0:T(8,128)S(1)} %bitcast.19), custom_call_target="tpu_custom_call" | custom-call | tf_op jit(solution)/shard_map/pallas_call | solution.py:105
  141.1 86.9 %reduce-scatter.2.cloned.1.call-done = f32[1024,128]{1,0:T(8,128)} async-done(((f32[8192,128]{1,0:T(8,128)}), f32[1024,128]{1,0:T(8,128)}) %reduce-scatter.2.cloned.1.call-update) | async-done | bytes 524304 | tf_op jit(solution)/shard_map/reduce_scatter | solution.py:141
  228.1 2.6 fusion.3
  230.7 1.2 collective-permute-done.4
  231.9 1.6 collective-permute-start.5
  233.5 2.8 collective-permute-done.5
  236.3 1.5 collective-permute-start.6
  237.8 2.8 collective-permute-done.6
  240.6 1.8 collective-permute-start.7
  242.4 2.6 collective-permute-done.7
  245.0 2.2 collective-permute-start.8
  247.2 3.0 %collective-permute-done.8 = f32[128,128]{0,1:T(8,128)S(1)} collective-permute-done((f32[128,128]{0,1:T(8,128)S(1)}, f32[128,128]{0,1:T(8,128)S(1)}, u32[]{:S(2)}, u32[]{:S(2)}) %collective-permute-start.8) | collective-permute-done | bytes 65568 | tf_op jit(solution)/shard_map/ppermute | solution.py:59
  250.3 11.7 %cholesky.17 = f32[128,128]{1,0:T(8,128)S(1)} custom-call(f32[128,128]{1,0:T(8,128)S(1)} %fusion.7), custom_call_target="Cholesky" | custom-call | tf_op jit(solution)/shard_map/jit(cholesky)/cholesky | solution.py:145
  263.4 9.8 %custom-call.6 = f32[1,128,128]{1,2,0:T(8,128)S(1)} custom-call(f32[1,128,128]{2,1,0:T(8,128)S(1)} %fusion.4), custom_call_target="InvertDiagBlocksLowerTriangular" | custom-call | tf_op jit(solution)/shard_map/triangular_solve | solution.py:146
  273.5 1.4 convolution_multiply_fusion
  (42 shorter events, 7.0 us)
Async XLA Ops:
  7.2 78.5 %all-gather.2.cloned.1.call-start = ((), (), s32[]{:S(2)}) async-start(), calls=%async_computation.1 | async-start | bytes 4718592 | tf_op jit(solution)/shard_map/all_gather | solution.py:128
  7.9 220.1 %reduce-scatter.2.cloned.1.call-start = ((), (), s32[]{:S(2)}) async-start(), calls=%async_computation.2 | async-start | bytes 4718592 | tf_op jit(solution)/shard_map/reduce_scatter | solution.py:141
  85.6 0.7 copy-start
  86.3 0.7 copy-start.2
  87.0 8.4 %copy-start.6 = (f32[1024,128]{1,0:T(8,128)S(1)}, f32[1024,128]{1,0:T(8,128)}, u32[]{:S(2)}) copy-start(f32[1024,128]{1,0:T(8,128)} %param.6) | copy-start | bytes 1572868
  95.7 2.9 %collective-permute-start = (f32[2048,128]{1,0:T(8,128)S(1)}, f32[2048,128]{1,0:T(8,128)}, u32[]{:S(2)}, u32[]{:S(2)}) collective-permute-start(f32[2048,128]{1,0:T(8,128)S(1)} %dynamic-slice_bitcast_fusion), channel_id=1, source_target_pairs={{0,1},{1,0},{2,3},{3,2},{4,5},{5,4},{6,7},{7,6},{8,9},{9,8},{10,11... | collective-permute-start | bytes 3145736 | tf_op jit(solution)/shard_map/ppermute | solution.py:43
  100.0 14.9 %collective-permute-start.1 = (f32[1024,128]{1,0:T(8,128)S(1)}, f32[1024,128]{1,0:T(8,128)S(1)}, u32[]{:S(2)}, u32[]{:S(2)}) collective-permute-start(f32[1024,128]{1,0:T(8,128)S(1)} %get-tuple-element.6), channel_id=1, source_target_pairs={{0,2},{1,3},{2,0},{3,1},{4,6},{5,7},{6,4},{7,5},{8,10},{9,11},{10,... | collective-permute-start | bytes 1572872 | tf_op jit(solution)/shard_map/ppermute | solution.py:48
  101.5 23.7 %collective-permute-start.2 = (f32[1024,128]{1,0:T(8,128)S(1)}, f32[1024,128]{1,0:T(8,128)S(1)}, u32[]{:S(2)}, u32[]{:S(2)}) collective-permute-start(f32[1024,128]{1,0:T(8,128)S(1)} %get-tuple-element.7), channel_id=1, source_target_pairs={{0,2},{1,3},{2,0},{3,1},{4,6},{5,7},{6,4},{7,5},{8,10},{9,11},{10,... | collective-permute-start | bytes 1572872 | tf_op jit(solution)/shard_map/ppermute | solution.py:48
  125.5 2.7 collective-permute-start.3
  128.2 1.0 copy-start.7
  129.2 2.0 copy-start.1
  129.2 2.1 copy-start.3
  141.1 133.8 %copy-start.4 = (f32[1024,128]{1,0:T(8,128)}, f32[1024,128]{1,0:T(8,128)S(1)}, u32[]{:S(2)}) copy-start(f32[1024,128]{1,0:T(8,128)S(1)} %constant_dynamic-slice_fusion) | copy-start | bytes 1572868
  228.0 45.4 %copy-start.5 = (f32[1024,128]{1,0:T(8,128)S(1)}, f32[1024,128]{1,0:T(8,128)}, u32[]{:S(2)}) copy-start(f32[1024,128]{1,0:T(8,128)} %reduce-scatter.2.cloned.1.call-done) | copy-start | bytes 1572868
  230.6 1.3 collective-permute-start.4
  231.9 4.3 %collective-permute-start.5 = (f32[128,128]{0,1:T(8,128)S(1)}, f32[128,128]{0,1:T(8,128)S(1)}, u32[]{:S(2)}, u32[]{:S(2)}) collective-permute-start(f32[128,128]{0,1:T(8,128)S(1)} %add.82), channel_id=1, source_target_pairs={{0,2},{1,3},{2,0},{3,1},{4,6},{5,7},{6,4},{7,5},{8,10},{9,11},{10,... | collective-permute-start | bytes 196616 | tf_op jit(solution)/shard_map/ppermute | solution.py:59
  236.3 4.3 %collective-permute-start.6 = (f32[128,128]{0,1:T(8,128)S(1)}, f32[128,128]{0,1:T(8,128)S(1)}, u32[]{:S(2)}, u32[]{:S(2)}) collective-permute-start(f32[128,128]{0,1:T(8,128)S(1)} %add.83), channel_id=1, source_target_pairs={{0,4},{1,5},{2,6},{3,7},{4,0},{5,1},{6,2},{7,3},{8,12},{9,13},{10,... | collective-permute-start | bytes 196616 | tf_op jit(solution)/shard_map/ppermute | solution.py:59
  240.6 4.3 %collective-permute-start.7 = (f32[128,128]{0,1:T(8,128)S(1)}, f32[128,128]{0,1:T(8,128)S(1)}, u32[]{:S(2)}, u32[]{:S(2)}) collective-permute-start(f32[128,128]{0,1:T(8,128)S(1)} %add.84), channel_id=1, source_target_pairs={{0,8},{1,9},{2,10},{3,11},{4,12},{5,13},{6,14},{7,15},{8,0},{9,1},... | collective-permute-start | bytes 196616 | tf_op jit(solution)/shard_map/ppermute | solution.py:59
  245.0 5.2 %collective-permute-start.8 = (f32[128,128]{0,1:T(8,128)S(1)}, f32[128,128]{0,1:T(8,128)S(1)}, u32[]{:S(2)}, u32[]{:S(2)}) collective-permute-start(f32[128,128]{0,1:T(8,128)S(1)} %add.85), channel_id=1, source_target_pairs={{0,16},{1,17},{2,18},{3,19},{4,20},{5,21},{6,22},{7,23},{8,24},{9,... | collective-permute-start | bytes 196616 | tf_op jit(solution)/shard_map/ppermute | solution.py:59
Sparse Core Ops, SparseCore 0:
  10.1 75.4 all-gather.1
  141.2 86.8 reduce-scatter.1

commit v6 on v5

--- a/solution.py
+++ b/solution.py
@@ -49,6 +49,39 @@
         step *= 2
     other = lax.ppermute(part, axis, [(i, i ^ 1) for i in range(n)])
     return jnp.roll(jnp.stack([part, other]), inner, axis=0).reshape(x.shape)
+
+
+def line_gather(piece, axis, n):
+    groups = n // 2
+    outer = lax.axis_index(axis) // 2
+    up = [(i, i + 2) for i in range(n) if i + 2 < n]
+    down = [(i, i - 2) for i in range(n) if i >= 2]
+    from_below, from_above = piece, piece
+    below, above = [], []
+    for _ in range(groups - 1):
+        from_below = lax.ppermute(from_below, axis, up)
+        from_above = lax.ppermute(from_above, axis, down)
+        below.append(from_below)
+        above.append(from_above)
+    line = jnp.stack(below[::-1] + [piece] + above)
+    return lax.dynamic_slice_in_dim(line, groups - 1 - outer, groups, 0)
+
+
+def split_route_gather(x, axis, n):
+    width = x.shape[1]
+    if n % 2 or width % 2:
+        return lax.all_gather(x, axis, axis=0, tiled=True)
+    inner = lax.axis_index(axis) % 2
+    swap = [(i, i ^ 1) for i in range(n)]
+    first, second = x[:, : width // 2], x[:, width // 2 :]
+    pair = jnp.roll(jnp.stack([first, lax.ppermute(first, axis, swap)]), inner, axis=0)
+    first_all = line_gather(pair, axis, n)
+    line = line_gather(second, axis, n)
+    second_all = jnp.roll(jnp.stack([line, lax.ppermute(line, axis, swap)], axis=1), inner, axis=1)
+    rows = n * x.shape[0]
+    return jnp.concatenate(
+        [first_all.reshape(rows, width // 2), second_all.reshape(rows, width // 2)], axis=1
+    )
 
 
 def butterfly_sum(x, axes, n):
@@ -125,7 +158,7 @@
     stripe_rows = local_rows * row_count
     stripe_blocks = stripe_rows // block_size
     answers = local_rows * row_count * col_count
-    stripe_probe = lax.all_gather(probe, "row", axis=0, tiled=True)
+    stripe_probe = split_route_gather(probe, "row", row_count)
     partial_value = slot_product(
         blocks, stripe_probe, block_row, block_col, counts, owner_rows, False
     )

time: 282 us -> 295 us (1.046)
  waiting for transfers between devices: 205 us -> 161 us
  starting transfers between devices: 9.46 us -> 47.5 us
  other arithmetic: 26.8 us -> 35.6 us
  local copies, waits for them, and re-layouts: 3.29 us -> 12 us
    all_gather x1 -> x0, waiting for transfers between devices: 76.3 us -> none  [shards(): stripe_probe = lax.all_gather(probe, 'row', axis=0, tiled=True)]
    ppermute x0 -> x14, starting transfers between devices: none -> 38.1 us  [the longest x6 25.9 us: line_gather(): from_below = lax.ppermute(from_below, axis, up)]
    ppermute x0 -> x14, waiting for transfers between devices: none -> 32 us  [the longest x6 19.1 us: line_gather(): from_below = lax.ppermute(from_below, axis, up)]
    concatenate x0 -> x3, other arithmetic: none -> 8.76 us  [the longest x1 6.61 us: split_route_gather(): jnp.concatenate([first_all.reshape(rows, width // 2), second_all.reshape(...]
    dynamic_slice x0 -> x4, local copies, waits for them, and re-layouts: none -> 6.88 us  [the longest x3 4.09 us: line_gather(): return lax.dynamic_slice_in_dim(line, groups - 1 - outer, groups, 0)]
  transfers between devices with their start and end apart: 11 -> 24, of which waited for: 11 -> 16; matrix products, arithmetic and copies ran while one was open for 0% -> 2% of each run, Pallas kernels for 0% -> 0%
where the time goes in v6:
time: 295 us; the launch traced here: 294 us
  waiting for transfers between devices  161 us (55%)
  starting transfers between devices  47.5 us (16%)
  other arithmetic  35.6 us (12%)
  Pallas kernels  18.3 us (6%)
  between operations  15.2 us (5%)
  local copies, waits for them, and re-layouts  12 us (4%)
  matrix products  4.22 us (1%)
    reduce_scatter x1, waiting for transfers between devices, shards(): lax.psum_scatter(w_partial, 'row', scatter_dimension=0, tiled=True)  87.9 us
    ppermute x6, starting transfers between devices, line_gather(): from_below = lax.ppermute(from_below, axis, up)  25.9 us
    ppermute x2, waiting for transfers between devices, pair_all_reduce(): part = jnp.concatenate([p + lax.ppermute(p, axis, pairs) for p in pieces])  23.2 us
    ppermute x6, waiting for transfers between devices, line_gather(): from_below = lax.ppermute(from_below, axis, up)  19.1 us
    pallas_call x2, Pallas kernels, slot_product(): pl.pallas_call(kernel, grid_spec=grid_spec, out_shape=jax.ShapeDtypeStruc...  18.3 us
    ppermute x5, waiting for transfers between devices, butterfly_sum(): x = x + lax.ppermute(x, axes, [(i, i ^ step) for i in range(n)])  12.4 us
    another operation x3, other arithmetic, shards(): lower = jnp.linalg.cholesky(gram)  12.4 us
    another operation x2, other arithmetic, shards(): lax.linalg.triangular_solve(lower, jnp.eye(lower.shape[0], dtype=lower.dt...  10.5 us
  transfers between devices with their start and end apart: 24, of which 16 were waited for; matrix products, arithmetic and copies ran while one was open for 2% of the time, Pallas kernels for 0%

profile of v6, /device:TPU:0, one launch (start us, length us, event | category | flops | bytes accessed | tf_op | source)
XLA Modules:
  0.0 293.8 jit_solution(13372149474181802639)
XLA Ops:
  8.8 3.0 %collective-permute-start = (f32[1024,64]{0,1:T(8,128)S(1)}, f32[1024,64]{0,1:T(8,128)S(1)}, u32[]{:S(2)}, u32[]{:S(2)}) collective-permute-start(f32[1024,64]{0,1:T(8,128)S(1)} %copy.20), channel_id=1, source_target_pairs={{0,4},{4,0},{8,12},{12,8},{16,20},{20,16},{24,28},{28,24},{1,5},{5... | collective-permute-start | bytes 786440 | tf_op jit(solution)/shard_map/ppermute | solution.py:77
  12.0 3.5 %collective-permute-start.7 = (f32[1024,64]{0,1:T(8,128)S(1)}, f32[1024,64]{0,1:T(8,128)S(1)}, u32[]{:S(2)}, u32[]{:S(2)}) collective-permute-start(f32[1024,64]{0,1:T(8,128)S(1)} %copy.21), channel_id=1, source_target_pairs={{0,8},{4,12},{8,16},{12,20},{16,24},{20,28},{1,9},{5,13},{9,17},{1... | collective-permute-start | bytes 786440 | tf_op jit(solution)/shard_map/ppermute | solution.py:62
  18.3 3.8 %collective-permute-start.1 = (f32[2,1024,64]{1,2,0:T(8,128)S(1)}, f32[2,1024,64]{1,2,0:T(8,128)S(1)}, u32[]{:S(2)}, u32[]{:S(2)}) collective-permute-start(f32[2,1024,64]{1,2,0:T(8,128)S(1)} %fusion.8), channel_id=1, source_target_pairs={{0,8},{4,12},{8,16},{12,20},{16,24},{20,28},{1,9},{5,13},{9,17},{1... | collective-permute-start | bytes 1572872 | tf_op jit(solution)/shard_map/ppermute | solution.py:62
  23.3 4.6 %collective-permute-start.8 = (f32[1024,64]{0,1:T(8,128)S(1)}, f32[1024,64]{0,1:T(8,128)S(1)}, u32[]{:S(2)}, u32[]{:S(2)}) collective-permute-start(f32[1024,64]{0,1:T(8,128)S(1)} %collective-permute-done.7), channel_id=1, source_target_pairs={{0,8},{4,12},{8,16},{12,20},{16,24},{20,28},{1,9},{5,13},{9,17},{1... | collective-permute-start | bytes 786440 | tf_op jit(solution)/shard_map/ppermute | solution.py:62
  29.2 8.7 %collective-permute-done.8 = f32[1024,64]{0,1:T(8,128)S(1)} collective-permute-done((f32[1024,64]{0,1:T(8,128)S(1)}, f32[1024,64]{0,1:T(8,128)S(1)}, u32[]{:S(2)}, u32[]{:S(2)}) %collective-permute-start.8) | collective-permute-done | bytes 262176 | tf_op jit(solution)/shard_map/ppermute | solution.py:62
  37.9 5.1 %collective-permute-start.9 = (f32[1024,64]{0,1:T(8,128)S(1)}, f32[1024,64]{0,1:T(8,128)}, u32[]{:S(2)}, u32[]{:S(2)}) collective-permute-start(f32[1024,64]{0,1:T(8,128)S(1)} %collective-permute-done.8), channel_id=1, source_target_pairs={{0,8},{4,12},{8,16},{12,20},{16,24},{20,28},{1,9},{5,13},{9,17},{1... | collective-permute-start | bytes 786440 | tf_op jit(solution)/shard_map/ppermute | solution.py:62
  45.7 4.6 %collective-permute-start.2 = (f32[2,1024,64]{1,2,0:T(8,128)S(1)}, f32[2,1024,64]{1,2,0:T(8,128)S(1)}, u32[]{:S(2)}, u32[]{:S(2)}) collective-permute-start(f32[2,1024,64]{1,2,0:T(8,128)S(1)} %collective-permute-done.1), channel_id=1, source_target_pairs={{0,8},{4,12},{8,16},{12,20},{16,24},{20,28},{1,9},{5,13},{9,17},{1... | collective-permute-start | bytes 1572872 | tf_op jit(solution)/shard_map/ppermute | solution.py:62
  52.6 6.5 %collective-permute-done.2 = f32[2,1024,64]{1,2,0:T(8,128)S(1)} collective-permute-done((f32[2,1024,64]{1,2,0:T(8,128)S(1)}, f32[2,1024,64]{1,2,0:T(8,128)S(1)}, u32[]{:S(2)}, u32[]{:S(2)}) %collective-permute-start.2) | collective-permute-done | bytes 524320 | tf_op jit(solution)/shard_map/ppermute | solution.py:62
  59.1 4.4 %collective-permute-start.3 = (f32[2,1024,64]{1,2,0:T(8,128)S(1)}, f32[2,1024,64]{1,2,0:T(8,128)S(1)}, u32[]{:S(2)}, u32[]{:S(2)}) collective-permute-start(f32[2,1024,64]{1,2,0:T(8,128)S(1)} %collective-permute-done.2), channel_id=1, source_target_pairs={{0,8},{4,12},{8,16},{12,20},{16,24},{20,28},{1,9},{5,13},{9,17},{1... | collective-permute-start | bytes 1572872 | tf_op jit(solution)/shard_map/ppermute | solution.py:62
  67.6 3.9 %collective-permute-done.3 = f32[2,1024,64]{1,2,0:T(8,128)S(1)} collective-permute-done((f32[2,1024,64]{1,2,0:T(8,128)S(1)}, f32[2,1024,64]{1,2,0:T(8,128)S(1)}, u32[]{:S(2)}, u32[]{:S(2)}) %collective-permute-start.3) | collective-permute-done | bytes 524320 | tf_op jit(solution)/shard_map/ppermute | solution.py:62
  71.9 6.3 %collective-permute-done.6 = f32[2,1024,64]{1,2,0:T(8,128)S(1)} collective-permute-done((f32[2,1024,64]{1,2,0:T(8,128)S(1)}, f32[2,1024,64]{1,2,0:T(8,128)S(1)}, u32[]{:S(2)}, u32[]{:S(2)}) %collective-permute-start.6) | collective-permute-done | bytes 524320 | tf_op jit(solution)/shard_map/ppermute | solution.py:63
  81.2 5.3 %collective-permute-done.13 = f32[4,1024,64]{1,2,0:T(8,128)} collective-permute-done((f32[4,1024,64]{1,2,0:T(8,128)}, f32[4,1024,64]{1,2,0:T(8,128)}, u32[]{:S(2)}, u32[]{:S(2)}) %collective-permute-start.13) | collective-permute-done | bytes 1048608 | tf_op jit(solution)/shard_map/ppermute | solution.py:80
  88.6 2.8 copy.15
  91.3 6.6 %pad_maximum_fusion.source_ref = f32[8192,128]{1,0:T(8,128)} fusion(f32[8192,64]{1,0:T(8,128)} %bitcast.59, f32[8192,64]{1,0:T(8,128)} %bitcast.58), kind=kLoop, calls=%fused_computation.4 | loop fusion | flops 1048576 | bytes 8388608 | tf_op jit(solution)/shard_map/concatenate | solution.py:82
  98.0 8.5 %shard_map.77 = f32[4096,128]{1,0:T(8,128)S(1)} custom-call(s32[128]{0:T(128)S(1)} %copy-done, s32[128]{0:T(128)S(1)} %copy-done.1, s32[1]{0:T(128)S(6)} %copy.35.count_ref, f32[128,128,128]{2,1,0:T(8,128)} %block_ref.3, f32[8192,128]{1,0:T(8,128)} %pad_maximum_fusion.source_ref), custom_call_target="tpu_custom_call" | custom-call | tf_op jit(solution)/shard_map/pallas_call | solution.py:138
  113.2 12.8 %collective-permute-done.15 = f32[1024,128]{1,0:T(8,128)S(1)} collective-permute-done((f32[1024,128]{1,0:T(8,128)S(1)}, f32[1024,128]{1,0:T(8,128)S(1)}, u32[]{:S(2)}, u32[]{:S(2)}) %collective-permute-start.15) | collective-permute-done | bytes 524320 | tf_op jit(solution)/shard_map/ppermute | solution.py:48
  125.9 10.4 %collective-permute-done.16 = f32[1024,128]{1,0:T(8,128)S(1)} collective-permute-done((f32[1024,128]{1,0:T(8,128)S(1)}, f32[1024,128]{1,0:T(8,128)S(1)}, u32[]{:S(2)}, u32[]{:S(2)}) %collective-permute-start.16) | collective-permute-done | bytes 524320 | tf_op jit(solution)/shard_map/ppermute | solution.py:48
  142.3 9.8 %shard_map.78 = f32[8192,128]{1,0:T(8,128)} custom-call(s32[128]{0:T(128)S(1)} %copy-done, s32[128]{0:T(128)S(1)} %copy-done.1, s32[1]{0:T(128)S(6)} %copy.35.count_ref, f32[128,128,128]{2,1,0:T(8,128)} %block_ref.3, f32[4096,128]{1,0:T(8,128)S(1)} %bitcast.54), custom_call_target="tpu_custom_call" | custom-call | tf_op jit(solution)/shard_map/pallas_call | solution.py:138
  152.2 87.9 %reduce-scatter.2.cloned.1.call-done = f32[1024,128]{1,0:T(8,128)} async-done(((f32[8192,128]{1,0:T(8,128)}), f32[1024,128]{1,0:T(8,128)}) %reduce-scatter.2.cloned.1.call-update) | async-done | bytes 524304 | tf_op jit(solution)/shard_map/reduce_scatter | solution.py:174
  245.6 2.8 collective-permute-done.19
  249.9 2.8 collective-permute-done.20
  259.3 3.0 %collective-permute-done.22 = f32[128,128]{0,1:T(8,128)S(1)} collective-permute-done((f32[128,128]{0,1:T(8,128)S(1)}, f32[128,128]{0,1:T(8,128)S(1)}, u32[]{:S(2)}, u32[]{:S(2)}) %collective-permute-start.22) | collective-permute-done | bytes 65568 | tf_op jit(solution)/shard_map/ppermute | solution.py:92
  262.4 11.7 %cholesky.17 = f32[128,128]{1,0:T(8,128)S(1)} custom-call(f32[128,128]{1,0:T(8,128)S(1)} %fusion.13), custom_call_target="Cholesky" | custom-call | tf_op jit(solution)/shard_map/jit(cholesky)/cholesky | solution.py:178
  275.5 9.8 %custom-call.6 = f32[1,128,128]{1,2,0:T(8,128)S(1)} custom-call(f32[1,128,128]{2,1,0:T(8,128)S(1)} %fusion.10), custom_call_target="InvertDiagBlocksLowerTriangular" | custom-call | tf_op jit(solution)/shard_map/triangular_solve | solution.py:179
  (88 shorter events, 50.1 us)
Async XLA Ops:
  7.2 233.0 %reduce-scatter.2.cloned.1.call-start = ((), (), s32[]{:S(2)}) async-start(), calls=%async_computation.1 | async-start | bytes 4718592 | tf_op jit(solution)/shard_map/reduce_scatter | solution.py:174
  8.8 9.3 %collective-permute-start = (f32[1024,64]{0,1:T(8,128)S(1)}, f32[1024,64]{0,1:T(8,128)S(1)}, u32[]{:S(2)}, u32[]{:S(2)}) collective-permute-start(f32[1024,64]{0,1:T(8,128)S(1)} %copy.20), channel_id=1, source_target_pairs={{0,4},{4,0},{8,12},{12,8},{16,20},{20,16},{24,28},{28,24},{1,5},{5... | collective-permute-start | bytes 786440 | tf_op jit(solution)/shard_map/ppermute | solution.py:77
  12.0 11.3 %collective-permute-start.7 = (f32[1024,64]{0,1:T(8,128)S(1)}, f32[1024,64]{0,1:T(8,128)S(1)}, u32[]{:S(2)}, u32[]{:S(2)}) collective-permute-start(f32[1024,64]{0,1:T(8,128)S(1)} %copy.21), channel_id=1, source_target_pairs={{0,8},{4,12},{8,16},{12,20},{16,24},{20,28},{1,9},{5,13},{9,17},{1... | collective-permute-start | bytes 786440 | tf_op jit(solution)/shard_map/ppermute | solution.py:62
  15.5 12.4 %collective-permute-start.10 = (f32[1024,64]{0,1:T(8,128)S(1)}, f32[1024,64]{0,1:T(8,128)S(1)}, u32[]{:S(2)}, u32[]{:S(2)}) collective-permute-start(f32[1024,64]{0,1:T(8,128)S(1)} %copy.21), channel_id=1, source_target_pairs={{8,0},{12,4},{16,8},{20,12},{24,16},{28,20},{9,1},{13,5},{17,9},{2... | collective-permute-start | bytes 786440 | tf_op jit(solution)/shard_map/ppermute | solution.py:63
  18.3 27.4 %collective-permute-start.1 = (f32[2,1024,64]{1,2,0:T(8,128)S(1)}, f32[2,1024,64]{1,2,0:T(8,128)S(1)}, u32[]{:S(2)}, u32[]{:S(2)}) collective-permute-start(f32[2,1024,64]{1,2,0:T(8,128)S(1)} %fusion.8), channel_id=1, source_target_pairs={{0,8},{4,12},{8,16},{12,20},{16,24},{20,28},{1,9},{5,13},{9,17},{1... | collective-permute-start | bytes 1572872 | tf_op jit(solution)/shard_map/ppermute | solution.py:62
  22.0 28.2 %collective-permute-start.4 = (f32[2,1024,64]{1,2,0:T(8,128)S(1)}, f32[2,1024,64]{1,2,0:T(8,128)S(1)}, u32[]{:S(2)}, u32[]{:S(2)}) collective-permute-start(f32[2,1024,64]{1,2,0:T(8,128)S(1)} %fusion.8), channel_id=1, source_target_pairs={{8,0},{12,4},{16,8},{20,12},{24,16},{28,20},{9,1},{13,5},{17,9},{2... | collective-permute-start | bytes 1572872 | tf_op jit(solution)/shard_map/ppermute | solution.py:63
  23.3 14.6 %collective-permute-start.8 = (f32[1024,64]{0,1:T(8,128)S(1)}, f32[1024,64]{0,1:T(8,128)S(1)}, u32[]{:S(2)}, u32[]{:S(2)}) collective-permute-start(f32[1024,64]{0,1:T(8,128)S(1)} %collective-permute-done.7), channel_id=1, source_target_pairs={{0,8},{4,12},{8,16},{12,20},{16,24},{20,28},{1,9},{5,13},{9,17},{1... | collective-permute-start | bytes 786440 | tf_op jit(solution)/shard_map/ppermute | solution.py:62
  27.9 16.4 %collective-permute-start.11 = (f32[1024,64]{0,1:T(8,128)S(1)}, f32[1024,64]{0,1:T(8,128)S(1)}, u32[]{:S(2)}, u32[]{:S(2)}) collective-permute-start(f32[1024,64]{0,1:T(8,128)S(1)} %collective-permute-done.10), channel_id=1, source_target_pairs={{8,0},{12,4},{16,8},{20,12},{24,16},{28,20},{9,1},{13,5},{17,9},{2... | collective-permute-start | bytes 786440 | tf_op jit(solution)/shard_map/ppermute | solution.py:63
  37.9 13.6 %collective-permute-start.9 = (f32[1024,64]{0,1:T(8,128)S(1)}, f32[1024,64]{0,1:T(8,128)}, u32[]{:S(2)}, u32[]{:S(2)}) collective-permute-start(f32[1024,64]{0,1:T(8,128)S(1)} %collective-permute-done.8), channel_id=1, source_target_pairs={{0,8},{4,12},{8,16},{12,20},{16,24},{20,28},{1,9},{5,13},{9,17},{1... | collective-permute-start | bytes 786440 | tf_op jit(solution)/shard_map/ppermute | solution.py:62
  44.4 19.2 %collective-permute-start.12 = (f32[1024,64]{0,1:T(8,128)S(1)}, f32[1024,64]{0,1:T(8,128)S(1)}, u32[]{:S(2)}, u32[]{:S(2)}) collective-permute-start(f32[1024,64]{0,1:T(8,128)S(1)} %collective-permute-done.11), channel_id=1, source_target_pairs={{8,0},{12,4},{16,8},{20,12},{24,16},{28,20},{9,1},{13,5},{17,9},{2... | collective-permute-start | bytes 786440 | tf_op jit(solution)/shard_map/ppermute | solution.py:63
  45.7 13.4 %collective-permute-start.2 = (f32[2,1024,64]{1,2,0:T(8,128)S(1)}, f32[2,1024,64]{1,2,0:T(8,128)S(1)}, u32[]{:S(2)}, u32[]{:S(2)}) collective-permute-start(f32[2,1024,64]{1,2,0:T(8,128)S(1)} %collective-permute-done.1), channel_id=1, source_target_pairs={{0,8},{4,12},{8,16},{12,20},{16,24},{20,28},{1,9},{5,13},{9,17},{1... | collective-permute-start | bytes 1572872 | tf_op jit(solution)/shard_map/ppermute | solution.py:62
  50.3 16.0 %collective-permute-start.5 = (f32[2,1024,64]{1,2,0:T(8,128)S(1)}, f32[2,1024,64]{1,2,0:T(8,128)S(1)}, u32[]{:S(2)}, u32[]{:S(2)}) collective-permute-start(f32[2,1024,64]{1,2,0:T(8,128)S(1)} %collective-permute-done.4), channel_id=1, source_target_pairs={{8,0},{12,4},{16,8},{20,12},{24,16},{28,20},{9,1},{13,5},{17,9},{2... | collective-permute-start | bytes 1572872 | tf_op jit(solution)/shard_map/ppermute | solution.py:63
  59.1 12.4 %collective-permute-start.3 = (f32[2,1024,64]{1,2,0:T(8,128)S(1)}, f32[2,1024,64]{1,2,0:T(8,128)S(1)}, u32[]{:S(2)}, u32[]{:S(2)}) collective-permute-start(f32[2,1024,64]{1,2,0:T(8,128)S(1)} %collective-permute-done.2), channel_id=1, source_target_pairs={{0,8},{4,12},{8,16},{12,20},{16,24},{20,28},{1,9},{5,13},{9,17},{1... | collective-permute-start | bytes 1572872 | tf_op jit(solution)/shard_map/ppermute | solution.py:62
  64.7 21.8 %collective-permute-start.13 = (f32[4,1024,64]{1,2,0:T(8,128)}, f32[4,1024,64]{1,2,0:T(8,128)}, u32[]{:S(2)}, u32[]{:S(2)}) collective-permute-start(f32[4,1024,64]{1,2,0:T(8,128)} %constant_dynamic-slice_fusion.1), channel_id=1, source_target_pairs={{0,4},{4,0},{8,12},{12,8},{16,20},{20,16},{24,28},{28,24},{1,5},{5... | collective-permute-start | bytes 3145736 | tf_op jit(solution)/shard_map/ppermute | solution.py:80
  66.3 11.9 %collective-permute-start.6 = (f32[2,1024,64]{1,2,0:T(8,128)S(1)}, f32[2,1024,64]{1,2,0:T(8,128)S(1)}, u32[]{:S(2)}, u32[]{:S(2)}) collective-permute-start(f32[2,1024,64]{1,2,0:T(8,128)S(1)} %collective-permute-done.5), channel_id=1, source_target_pairs={{8,0},{12,4},{16,8},{20,12},{24,16},{28,20},{9,1},{13,5},{17,9},{2... | collective-permute-start | bytes 1572872 | tf_op jit(solution)/shard_map/ppermute | solution.py:63
  106.8 2.9 collective-permute-start.14
  111.1 14.9 %collective-permute-start.15 = (f32[1024,128]{1,0:T(8,128)S(1)}, f32[1024,128]{1,0:T(8,128)S(1)}, u32[]{:S(2)}, u32[]{:S(2)}) collective-permute-start(f32[1024,128]{1,0:T(8,128)S(1)} %get-tuple-element.6), channel_id=1, source_target_pairs={{0,2},{1,3},{2,0},{3,1},{4,6},{5,7},{6,4},{7,5},{8,10},{9,11},{10,... | collective-permute-start | bytes 1572872 | tf_op jit(solution)/shard_map/ppermute | solution.py:48
  112.7 23.7 %collective-permute-start.16 = (f32[1024,128]{1,0:T(8,128)S(1)}, f32[1024,128]{1,0:T(8,128)S(1)}, u32[]{:S(2)}, u32[]{:S(2)}) collective-permute-start(f32[1024,128]{1,0:T(8,128)S(1)} %get-tuple-element.7), channel_id=1, source_target_pairs={{0,2},{1,3},{2,0},{3,1},{4,6},{5,7},{6,4},{7,5},{8,10},{9,11},{10,... | collective-permute-start | bytes 1572872 | tf_op jit(solution)/shard_map/ppermute | solution.py:48
  136.6 2.7 collective-permute-start.17
  242.7 1.3 collective-permute-start.18
  244.0 4.3 %collective-permute-start.19 = (f32[128,128]{0,1:T(8,128)S(1)}, f32[128,128]{0,1:T(8,128)S(1)}, u32[]{:S(2)}, u32[]{:S(2)}) collective-permute-start(f32[128,128]{0,1:T(8,128)S(1)} %add.108), channel_id=1, source_target_pairs={{0,2},{1,3},{2,0},{3,1},{4,6},{5,7},{6,4},{7,5},{8,10},{9,11},{10,... | collective-permute-start | bytes 196616 | tf_op jit(solution)/shard_map/ppermute | solution.py:92
  248.4 4.3 %collective-permute-start.20 = (f32[128,128]{0,1:T(8,128)S(1)}, f32[128,128]{0,1:T(8,128)S(1)}, u32[]{:S(2)}, u32[]{:S(2)}) collective-permute-start(f32[128,128]{0,1:T(8,128)S(1)} %add.109), channel_id=1, source_target_pairs={{0,4},{1,5},{2,6},{3,7},{4,0},{5,1},{6,2},{7,3},{8,12},{9,13},{10,... | collective-permute-start | bytes 196616 | tf_op jit(solution)/shard_map/ppermute | solution.py:92
  252.7 4.3 %collective-permute-start.21 = (f32[128,128]{0,1:T(8,128)S(1)}, f32[128,128]{0,1:T(8,128)S(1)}, u32[]{:S(2)}, u32[]{:S(2)}) collective-permute-start(f32[128,128]{0,1:T(8,128)S(1)} %add.110), channel_id=1, source_target_pairs={{0,8},{1,9},{2,10},{3,11},{4,12},{5,13},{6,14},{7,15},{8,0},{9,1},... | collective-permute-start | bytes 196616 | tf_op jit(solution)/shard_map/ppermute | solution.py:92
  257.1 5.2 %collective-permute-start.22 = (f32[128,128]{0,1:T(8,128)S(1)}, f32[128,128]{0,1:T(8,128)S(1)}, u32[]{:S(2)}, u32[]{:S(2)}) collective-permute-start(f32[128,128]{0,1:T(8,128)S(1)} %add.111), channel_id=1, source_target_pairs={{0,16},{1,17},{2,18},{3,19},{4,20},{5,21},{6,22},{7,23},{8,24},{9,... | collective-permute-start | bytes 196616 | tf_op jit(solution)/shard_map/ppermute | solution.py:92
  (6 other events, 202.9 us)
Sparse Core Ops, SparseCore 0:
  152.3 87.8 reduce-scatter.1

commit v7 on v3

--- a/solution.py
+++ b/solution.py
@@ -10,6 +10,7 @@
 PRECISE = lax.Precision.HIGHEST
 INTERPRET = False
 KERNEL_PRECISION = lax.Precision.HIGH
+ACCUMULATORS = 4
 
 
 def shift_pairs(n, k):
@@ -63,22 +64,27 @@
     slot_count, block_size = blocks.shape[0], blocks.shape[1]
     width = source.shape[1]
     group = 32 if slot_count % 32 == 0 else 1
+    lanes = ACCUMULATORS if group % ACCUMULATORS == 0 else 1
 
-    def kernel(row_ref, col_ref, count_ref, block_ref, source_ref, out_ref):
+    def kernel(row_ref, col_ref, count_ref, block_ref, source_ref, out_ref, *sums):
         step = pl.program_id(0)
 
         @pl.when(step == 0)
         def _():
-            out_ref[...] = jnp.zeros_like(out_ref)
+            for acc in sums:
+                acc[...] = jnp.zeros_like(acc)
 
-        def body(s, carry):
-            slot = step * group + s
-            read = row_ref[slot] if transpose else col_ref[slot]
-            write = col_ref[slot] if transpose else row_ref[slot]
-
-            @pl.when(slot < count_ref[0])
-            def _():
-                piece = source_ref[pl.ds(pl.multiple_of(read * block_size, block_size), block_size), :]
+        def body(t, carry):
+            for lane in range(lanes):
+                s = t * lanes + lane
+                slot = step * group + s
+                read = row_ref[slot] if transpose else col_ref[slot]
+                write = col_ref[slot] if transpose else row_ref[slot]
+                read = jnp.clip(read, 0, source_ref.shape[0] // block_size - 1)
+                write = jnp.clip(write, 0, out_ref.shape[0] // block_size - 1)
+                live = (slot < count_ref[0]).astype(jnp.float32)
+                at_read = pl.ds(pl.multiple_of(read * block_size, block_size), block_size)
+                piece = source_ref[at_read, :]
                 block = block_ref[s]
                 if transpose:
                     block = block.T
@@ -86,11 +92,18 @@
                     block, piece, precision=KERNEL_PRECISION, preferred_element_type=jnp.float32
                 )
                 at = pl.ds(pl.multiple_of(write * block_size, block_size), block_size)
-                out_ref[at, :] = out_ref[at, :] + product
-
+                acc = sums[lane]
+                acc[at, :] = acc[at, :] + product * live
             return carry
 
-        lax.fori_loop(0, group, body, 0, unroll=True)
+        lax.fori_loop(0, group // lanes, body, 0, unroll=True)
+
+        @pl.when(step == pl.num_programs(0) - 1)
+        def _():
+            total = sums[0][...]
+            for acc in sums[1:]:
+                total = total + acc[...]
+            out_ref[...] = total
 
     grid_spec = pltpu.PrefetchScalarGridSpec(
         num_scalar_prefetch=3,
@@ -100,13 +113,14 @@
             pl.BlockSpec(source.shape, lambda g, *_: (0, 0)),
         ],
         out_specs=pl.BlockSpec((out_rows, width), lambda g, *_: (0, 0)),
+        scratch_shapes=[pltpu.VMEM((out_rows, width), jnp.float32) for _ in range(lanes)],
     )
     return pl.pallas_call(
         kernel,
         grid_spec=grid_spec,
         out_shape=jax.ShapeDtypeStruct((out_rows, width), jnp.float32),
         compiler_params=pltpu.CompilerParams(
-            dimension_semantics=("arbitrary",), vmem_limit_bytes=48 * 1024 * 1024
+            dimension_semantics=("arbitrary",), vmem_limit_bytes=56 * 1024 * 1024
         ),
         interpret=INTERPRET,
     )(block_row, block_col, counts, blocks, source)

time: 322 us -> 287 us (0.89)
  Pallas kernels: 59.1 us -> 22.5 us
    pallas_call x2, Pallas kernels: 59.1 us -> 22.5 us  [slot_product(): pl.pallas_call(kernel, grid_spec=grid_spec, out_shape=jax.ShapeDtypeStruc...]
  transfers between devices with their start and end apart: 10 -> 10, of which waited for: 10 -> 10; matrix products, arithmetic and copies ran while one was open for 0% -> 1% of each run, Pallas kernels for 0% -> 0%
where the time goes in v7:
time: 287 us; the launch traced here: 286 us
  waiting for transfers between devices  204 us (71%)
  other arithmetic  28.1 us (10%)
  Pallas kernels  22.5 us (8%)
  between operations  14.9 us (5%)
  starting transfers between devices  8.87 us (3%)
  matrix products  3.97 us (1%)
  local copies, waits for them, and re-layouts  3.32 us (1%)
    reduce_scatter x1, waiting for transfers between devices, shards(): lax.psum_scatter(w_partial, 'row', scatter_dimension=0, tiled=True)  85.9 us
    all_gather x1, waiting for transfers between devices, shards(): stripe_probe = lax.all_gather(probe, 'row', axis=0, tiled=True)  76.3 us
    ppermute x1, waiting for transfers between devices, pair_all_reduce(): part = part + lax.ppermute(part, axis, [(i, i ^ step) for i in range(n)])  23.7 us
    pallas_call x2, Pallas kernels, slot_product(): pl.pallas_call(kernel, grid_spec=grid_spec, out_shape=jax.ShapeDtypeStruc...  22.5 us
    ppermute x5, waiting for transfers between devices, butterfly_sum(): x = x + lax.ppermute(x, axes, [(i, i ^ step) for i in range(n)])  12.4 us
    another operation x3, other arithmetic, shards(): lower = jnp.linalg.cholesky(gram)  12.4 us
    another operation x2, other arithmetic, shards(): lax.linalg.triangular_solve(lower, sketch, left_side=False, lower=True, t...  10.5 us
    ppermute x5, starting transfers between devices, butterfly_sum(): x = x + lax.ppermute(x, axes, [(i, i ^ step) for i in range(n)])  7.12 us
  transfers between devices with their start and end apart: 10, of which 10 were waited for; matrix products, arithmetic and copies ran while one was open for 1% of the time, Pallas kernels for 0%

profile of v7, /device:TPU:0, one launch (start us, length us, event | category | flops | bytes accessed | tf_op | source)
XLA Modules:
  0.0 286.2 jit_solution(11995188679702912989)
XLA Ops:
  9.3 76.3 %all-gather.2.cloned.1.call-done.source_ref = f32[8192,128]{1,0:T(8,128)} async-done(((f32[1024,128]{1,0:T(8,128)}), f32[8192,128]{1,0:T(8,128)}) %all-gather.2.cloned.1.call-update) | async-done | bytes 4194320 | tf_op jit(solution)/shard_map/all_gather | solution.py:141
  85.6 10.7 %shard_map.77 = f32[4096,128]{1,0:T(8,128)} custom-call(s32[128]{0:T(128)} %row_ref.3, s32[128]{0:T(128)} %col_ref.3, s32[1]{0:T(128)S(6)} %copy.13.count_ref, f32[128,128,128]{2,1,0:T(8,128)} %block_ref.3, f32[8192,128]{1,0:T(8,128)} %all-gather.2.cloned.1.call-done.source_ref), custom_call_target="tpu_custom_call" | custom-call | tf_op jit(solution)/shard_map/pallas_call | solution.py:118
  96.3 2.1 add_dynamic-update-slice_fusion
  98.4 1.4 dynamic-slice_bitcast_fusion
  99.9 2.8 collective-permute-done
  102.7 1.3 bitcast_add_fusion
  104.0 1.5 collective-permute-start.1
  105.6 23.7 %collective-permute-done.1 = f32[2048,128]{1,0:T(8,128)S(1)} collective-permute-done((f32[2048,128]{1,0:T(8,128)S(1)}, f32[2048,128]{1,0:T(8,128)S(1)}, u32[]{:S(2)}, u32[]{:S(2)}) %collective-permute-start.1) | collective-permute-done | bytes 1048608 | tf_op jit(solution)/shard_map/ppermute | solution.py:47
  129.5 2.6 collective-permute-done.2
  132.1 1.7 fusion.2
  133.9 11.8 %shard_map.78 = f32[8192,128]{1,0:T(8,128)} custom-call(s32[128]{0:T(128)} %row_ref.3, s32[128]{0:T(128)} %col_ref.3, s32[1]{0:T(128)S(6)} %copy.13.count_ref, f32[128,128,128]{2,1,0:T(8,128)} %block_ref.3, f32[4096,128]{1,0:T(8,128)} %bitcast.17), custom_call_target="tpu_custom_call" | custom-call | tf_op jit(solution)/shard_map/pallas_call | solution.py:118
  146.8 85.9 %reduce-scatter.2.cloned.1.call-done = f32[1024,128]{1,0:T(8,128)} async-done(((f32[8192,128]{1,0:T(8,128)}), f32[1024,128]{1,0:T(8,128)}) %reduce-scatter.2.cloned.1.call-update) | async-done | bytes 524304 | tf_op jit(solution)/shard_map/reduce_scatter | solution.py:154
  232.7 2.6 fusion.3
  236.6 1.5 collective-permute-start.4
  238.2 2.8 collective-permute-done.4
  241.0 1.5 collective-permute-start.5
  242.5 2.8 collective-permute-done.5
  245.3 1.8 collective-permute-start.6
  247.1 2.6 collective-permute-done.6
  249.7 2.2 collective-permute-start.7
  251.9 3.0 %collective-permute-done.7 = f32[128,128]{0,1:T(8,128)S(1)} collective-permute-done((f32[128,128]{0,1:T(8,128)S(1)}, f32[128,128]{0,1:T(8,128)S(1)}, u32[]{:S(2)}, u32[]{:S(2)}) %collective-permute-start.7) | collective-permute-done | bytes 65568 | tf_op jit(solution)/shard_map/ppermute | solution.py:58
  255.0 11.7 %cholesky.16 = f32[128,128]{1,0:T(8,128)S(1)} custom-call(f32[128,128]{1,0:T(8,128)S(1)} %fusion.6), custom_call_target="Cholesky" | custom-call | tf_op jit(solution)/shard_map/jit(cholesky)/cholesky | solution.py:158
  268.1 9.8 %custom-call.6 = f32[1,128,128]{1,2,0:T(8,128)S(1)} custom-call(f32[1,128,128]{2,1,0:T(8,128)S(1)} %fusion.4), custom_call_target="InvertDiagBlocksLowerTriangular" | custom-call | tf_op jit(solution)/shard_map/triangular_solve | solution.py:159
  277.9 1.4 convolution_multiply_fusion
  (29 shorter events, 5.6 us)
Async XLA Ops:
  7.2 78.5 %all-gather.2.cloned.1.call-start = ((), (), s32[]{:S(2)}) async-start(), calls=%async_computation.1 | async-start | bytes 4718592 | tf_op jit(solution)/shard_map/all_gather | solution.py:141
  7.9 224.8 %reduce-scatter.2.cloned.1.call-start = ((), (), s32[]{:S(2)}) async-start(), calls=%async_computation.2 | async-start | bytes 4718592 | tf_op jit(solution)/shard_map/reduce_scatter | solution.py:154
  9.3 87.0 %copy-start.3 = (f32[1024,128]{1,0:T(8,128)S(1)}, f32[1024,128]{1,0:T(8,128)}, u32[]{:S(2)}) copy-start(f32[1024,128]{1,0:T(8,128)} %param.6) | copy-start | bytes 1572868
  98.4 4.3 %copy-start = (f32[4096,128]{1,0:T(8,128)S(1)}, f32[4096,128]{1,0:T(8,128)}, u32[]{:S(2)}) copy-start(f32[4096,128]{1,0:T(8,128)} %add_dynamic-update-slice_fusion) | copy-start | bytes 6291460
  99.8 2.9 collective-permute-start
  104.0 25.3 %collective-permute-start.1 = (f32[2048,128]{1,0:T(8,128)S(1)}, f32[2048,128]{1,0:T(8,128)S(1)}, u32[]{:S(2)}, u32[]{:S(2)}) collective-permute-start(f32[2048,128]{1,0:T(8,128)S(1)} %bitcast_add_fusion), channel_id=1, source_target_pairs={{0,2},{1,3},{2,0},{3,1},{4,6},{5,7},{6,4},{7,5},{8,10},{9,11},{10,... | collective-permute-start | bytes 3145736 | tf_op jit(solution)/shard_map/ppermute | solution.py:47
  129.4 2.7 collective-permute-start.2
  146.8 132.5 %copy-start.1 = (f32[1024,128]{1,0:T(8,128)}, f32[1024,128]{1,0:T(8,128)S(1)}, u32[]{:S(2)}) copy-start(f32[1024,128]{1,0:T(8,128)S(1)} %constant_dynamic-slice_fusion) | copy-start | bytes 1572868
  232.7 45.2 %copy-start.2 = (f32[1024,128]{1,0:T(8,128)S(1)}, f32[1024,128]{1,0:T(8,128)}, u32[]{:S(2)}) copy-start(f32[1024,128]{1,0:T(8,128)} %reduce-scatter.2.cloned.1.call-done) | copy-start | bytes 1572868
  235.3 1.3 collective-permute-start.3
  236.6 4.3 %collective-permute-start.4 = (f32[128,128]{0,1:T(8,128)S(1)}, f32[128,128]{0,1:T(8,128)S(1)}, u32[]{:S(2)}, u32[]{:S(2)}) collective-permute-start(f32[128,128]{0,1:T(8,128)S(1)} %add.78), channel_id=1, source_target_pairs={{0,2},{1,3},{2,0},{3,1},{4,6},{5,7},{6,4},{7,5},{8,10},{9,11},{10,... | collective-permute-start | bytes 196616 | tf_op jit(solution)/shard_map/ppermute | solution.py:58
  241.0 4.3 %collective-permute-start.5 = (f32[128,128]{0,1:T(8,128)S(1)}, f32[128,128]{0,1:T(8,128)S(1)}, u32[]{:S(2)}, u32[]{:S(2)}) collective-permute-start(f32[128,128]{0,1:T(8,128)S(1)} %add.79), channel_id=1, source_target_pairs={{0,4},{1,5},{2,6},{3,7},{4,0},{5,1},{6,2},{7,3},{8,12},{9,13},{10,... | collective-permute-start | bytes 196616 | tf_op jit(solution)/shard_map/ppermute | solution.py:58
  245.3 4.3 %collective-permute-start.6 = (f32[128,128]{0,1:T(8,128)S(1)}, f32[128,128]{0,1:T(8,128)S(1)}, u32[]{:S(2)}, u32[]{:S(2)}) collective-permute-start(f32[128,128]{0,1:T(8,128)S(1)} %add.80), channel_id=1, source_target_pairs={{0,8},{1,9},{2,10},{3,11},{4,12},{5,13},{6,14},{7,15},{8,0},{9,1},... | collective-permute-start | bytes 196616 | tf_op jit(solution)/shard_map/ppermute | solution.py:58
  249.7 5.2 %collective-permute-start.7 = (f32[128,128]{0,1:T(8,128)S(1)}, f32[128,128]{0,1:T(8,128)S(1)}, u32[]{:S(2)}, u32[]{:S(2)}) collective-permute-start(f32[128,128]{0,1:T(8,128)S(1)} %add.81), channel_id=1, source_target_pairs={{0,16},{1,17},{2,18},{3,19},{4,20},{5,21},{6,22},{7,23},{8,24},{9,... | collective-permute-start | bytes 196616 | tf_op jit(solution)/shard_map/ppermute | solution.py:58
Sparse Core Ops, SparseCore 0:
  10.1 75.4 all-gather.1
  145.9 86.8 reduce-scatter.1

commit v8 on v4

--- a/solution.py
+++ b/solution.py
@@ -62,7 +62,7 @@
 def slot_product(blocks, source, block_row, block_col, counts, out_rows, transpose):
     slot_count, block_size = blocks.shape[0], blocks.shape[1]
     width = source.shape[1]
-    group = 32 if slot_count % 32 == 0 else 1
+    group = 16 if slot_count % 16 == 0 else 1
 
     def kernel(row_ref, col_ref, count_ref, block_ref, source_ref, out_ref):
         step = pl.program_id(0)
@@ -140,7 +140,7 @@
     sketch = local_weight[:, None] * projected + w_share
     gram_part = jnp.dot(sketch.T, sketch, precision=PRECISE, preferred_element_type=jnp.float32)
     gram = butterfly_sum(gram_part, ("row", "col"), row_count * col_count)
-    lower = jnp.linalg.cholesky(gram)
+    lower = lax.linalg.cholesky(gram, symmetrize_input=False)
     solved = lax.linalg.triangular_solve(
         lower, sketch, left_side=False, lower=True, transpose_a=True
     )

time: 282 us -> 285 us (1.011)
  Pallas kernels: 18.1 us -> 21.7 us
    pallas_call x2, Pallas kernels: 18.1 us -> 21.7 us  [slot_product(): pl.pallas_call(kernel, grid_spec=grid_spec, out_shape=jax.ShapeDtypeStruc...]
where the time goes in v8:
time: 285 us
  waiting for transfers between devices  205 us (72%)
  other arithmetic  26.5 us (9%)
  Pallas kernels  21.7 us (8%)
  between operations  14.9 us (5%)
  starting transfers between devices  8.88 us (3%)
  matrix products  3.98 us (1%)
  local copies, waits for them, and re-layouts  3.11 us (1%)
    reduce_scatter x1, waiting for transfers between devices, shards(): lax.psum_scatter(w_partial, 'row', scatter_dimension=0, tiled=True)  86.9 us
    all_gather x1, waiting for transfers between devices, shards(): stripe_probe = lax.all_gather(probe, 'row', axis=0, tiled=True)  76.3 us
    ppermute x1, waiting for transfers between devices, pair_all_reduce(): part = part + lax.ppermute(part, axis, [(i, i ^ step) for i in range(n)])  23.7 us
    pallas_call x2, Pallas kernels, slot_product(): pl.pallas_call(kernel, grid_spec=grid_spec, out_shape=jax.ShapeDtypeStruc...  21.7 us
    ppermute x5, waiting for transfers between devices, butterfly_sum(): x = x + lax.ppermute(x, axes, [(i, i ^ step) for i in range(n)])  12.4 us
    another operation x3, other arithmetic, shards(): lower = lax.linalg.cholesky(gram, symmetrize_input=False)  12.4 us
    another operation x2, other arithmetic, shards(): lax.linalg.triangular_solve(lower, sketch, left_side=False, lower=True, t...  10.5 us
    ppermute x5, starting transfers between devices, butterfly_sum(): x = x + lax.ppermute(x, axes, [(i, i ^ step) for i in range(n)])  7.1 us
  transfers between devices with their start and end apart: 10, of which 10 were waited for; matrix products, arithmetic and copies ran while one was open for 0% of the time, Pallas kernels for 0%

profile of v8, /device:TPU:0, one launch (start us, length us, event | category | flops | bytes accessed | tf_op | source)
XLA Modules:
  0.0 284.6 jit_solution(9580204222864737463)
XLA Ops:
  9.3 76.3 %all-gather.2.cloned.1.call-done.source_ref = f32[8192,128]{1,0:T(8,128)} async-done(((f32[1024,128]{1,0:T(8,128)}), f32[8192,128]{1,0:T(8,128)}) %all-gather.2.cloned.1.call-update) | async-done | bytes 4194320 | tf_op jit(solution)/shard_map/all_gather | solution.py:126
  87.0 10.2 %shard_map.77 = f32[4096,128]{1,0:T(8,128)S(1)} custom-call(s32[128]{0:T(128)S(1)} %copy-done, s32[128]{0:T(128)S(1)} %copy-done.2, s32[1]{0:T(128)S(6)} %copy.9.count_ref, f32[128,128,128]{2,1,0:T(8,128)} %block_ref.3, f32[8192,128]{1,0:T(8,128)} %all-gather.2.cloned.1.call-done.source_ref), custom_call_target="tpu_custom_call" | custom-call | tf_op jit(solution)/shard_map/pallas_call | solution.py:103
  97.6 2.8 collective-permute-done
  100.4 1.3 bitcast_add_fusion
  101.7 1.6 collective-permute-start.1
  103.3 23.7 %collective-permute-done.1 = f32[2048,128]{1,0:T(8,128)S(1)} collective-permute-done((f32[2048,128]{1,0:T(8,128)S(1)}, f32[2048,128]{1,0:T(8,128)S(1)}, u32[]{:S(2)}, u32[]{:S(2)}) %collective-permute-start.1) | collective-permute-done | bytes 1048608 | tf_op jit(solution)/shard_map/ppermute | solution.py:46
  127.2 2.6 collective-permute-done.2
  129.8 1.0 copy-done.7
  130.8 2.0 fusion.2
  132.8 11.4 %shard_map.78 = f32[8192,128]{1,0:T(8,128)} custom-call(s32[128]{0:T(128)S(1)} %copy-done.1, s32[128]{0:T(128)S(1)} %copy-done.3, s32[1]{0:T(128)S(6)} %copy.9.count_ref, f32[128,128,128]{2,1,0:T(8,128)} %block_ref.3, f32[4096,128]{1,0:T(8,128)S(1)} %bitcast.13), custom_call_target="tpu_custom_call" | custom-call | tf_op jit(solution)/shard_map/pallas_call | solution.py:103
  144.3 86.9 %reduce-scatter.2.cloned.1.call-done = f32[1024,128]{1,0:T(8,128)} async-done(((f32[8192,128]{1,0:T(8,128)}), f32[1024,128]{1,0:T(8,128)}) %reduce-scatter.2.cloned.1.call-update) | async-done | bytes 524304 | tf_op jit(solution)/shard_map/reduce_scatter | solution.py:139
  231.2 2.6 fusion.3
  233.9 1.2 collective-permute-done.3
  235.1 1.5 collective-permute-start.4
  236.7 2.8 collective-permute-done.4
  239.5 1.5 collective-permute-start.5
  241.0 2.8 collective-permute-done.5
  243.8 1.8 collective-permute-start.6
  245.6 2.6 collective-permute-done.6
  248.2 2.2 collective-permute-start.7
  250.4 3.0 %collective-permute-done.7 = f32[128,128]{1,0:T(8,128)S(1)} collective-permute-done((f32[128,128]{1,0:T(8,128)S(1)}, f32[128,128]{1,0:T(8,128)S(1)}, u32[]{:S(2)}, u32[]{:S(2)}) %collective-permute-start.7) | collective-permute-done | bytes 65568 | tf_op jit(solution)/shard_map/ppermute | solution.py:57
  253.4 11.7 %cholesky.16 = f32[128,128]{1,0:T(8,128)S(1)} custom-call(f32[128,128]{1,0:T(8,128)S(1)} %add.77), custom_call_target="Cholesky" | custom-call | tf_op jit(solution)/shard_map/cholesky | solution.py:143
  266.5 9.8 %custom-call.5 = f32[1,128,128]{1,2,0:T(8,128)S(1)} custom-call(f32[1,128,128]{2,1,0:T(8,128)S(1)} %fusion.4), custom_call_target="InvertDiagBlocksLowerTriangular" | custom-call | tf_op jit(solution)/shard_map/triangular_solve | solution.py:144
  276.3 1.4 convolution_multiply_fusion
  (35 shorter events, 4.9 us)
Async XLA Ops:
  7.2 78.5 %all-gather.2.cloned.1.call-start = ((), (), s32[]{:S(2)}) async-start(), calls=%async_computation.1 | async-start | bytes 4718592 | tf_op jit(solution)/shard_map/all_gather | solution.py:126
  7.9 223.3 %reduce-scatter.2.cloned.1.call-start = ((), (), s32[]{:S(2)}) async-start(), calls=%async_computation.2 | async-start | bytes 4718592 | tf_op jit(solution)/shard_map/reduce_scatter | solution.py:139
  85.6 0.7 copy-start
  86.3 0.7 copy-start.2
  87.0 10.2 %copy-start.6 = (f32[1024,128]{1,0:T(8,128)S(1)}, f32[1024,128]{1,0:T(8,128)}, u32[]{:S(2)}) copy-start(f32[1024,128]{1,0:T(8,128)} %param.6) | copy-start | bytes 1572868
  97.5 2.9 %collective-permute-start = (f32[2048,128]{1,0:T(8,128)S(1)}, f32[2048,128]{1,0:T(8,128)}, u32[]{:S(2)}, u32[]{:S(2)}) collective-permute-start(f32[2048,128]{1,0:T(8,128)S(1)} %dynamic-slice_bitcast_fusion), channel_id=1, source_target_pairs={{0,1},{1,0},{2,3},{3,2},{4,5},{5,4},{6,7},{7,6},{8,9},{9,8},{10,11... | collective-permute-start | bytes 3145736 | tf_op jit(solution)/shard_map/ppermute | solution.py:43
  101.7 25.3 %collective-permute-start.1 = (f32[2048,128]{1,0:T(8,128)S(1)}, f32[2048,128]{1,0:T(8,128)S(1)}, u32[]{:S(2)}, u32[]{:S(2)}) collective-permute-start(f32[2048,128]{1,0:T(8,128)S(1)} %bitcast_add_fusion), channel_id=1, source_target_pairs={{0,2},{1,3},{2,0},{3,1},{4,6},{5,7},{6,4},{7,5},{8,10},{9,11},{10,... | collective-permute-start | bytes 3145736 | tf_op jit(solution)/shard_map/ppermute | solution.py:46
  127.1 2.7 collective-permute-start.2
  129.8 1.0 copy-start.7
  130.8 2.0 copy-start.1
  130.8 2.0 copy-start.3
  144.3 133.4 %copy-start.4 = (f32[1024,128]{1,0:T(8,128)}, f32[1024,128]{1,0:T(8,128)S(1)}, u32[]{:S(2)}) copy-start(f32[1024,128]{1,0:T(8,128)S(1)} %constant_dynamic-slice_fusion) | copy-start | bytes 1572868
  231.2 45.0 %copy-start.5 = (f32[1024,128]{1,0:T(8,128)S(1)}, f32[1024,128]{1,0:T(8,128)}, u32[]{:S(2)}) copy-start(f32[1024,128]{1,0:T(8,128)} %reduce-scatter.2.cloned.1.call-done) | copy-start | bytes 1572868
  233.8 1.3 collective-permute-start.3
  235.1 4.3 %collective-permute-start.4 = (f32[128,128]{1,0:T(8,128)S(1)}, f32[128,128]{1,0:T(8,128)S(1)}, u32[]{:S(2)}, u32[]{:S(2)}) collective-permute-start(f32[128,128]{1,0:T(8,128)S(1)} %add.73), channel_id=1, source_target_pairs={{0,2},{1,3},{2,0},{3,1},{4,6},{5,7},{6,4},{7,5},{8,10},{9,11},{10,... | collective-permute-start | bytes 196616 | tf_op jit(solution)/shard_map/ppermute | solution.py:57
  239.5 4.3 %collective-permute-start.5 = (f32[128,128]{1,0:T(8,128)S(1)}, f32[128,128]{1,0:T(8,128)S(1)}, u32[]{:S(2)}, u32[]{:S(2)}) collective-permute-start(f32[128,128]{1,0:T(8,128)S(1)} %add.74), channel_id=1, source_target_pairs={{0,4},{1,5},{2,6},{3,7},{4,0},{5,1},{6,2},{7,3},{8,12},{9,13},{10,... | collective-permute-start | bytes 196616 | tf_op jit(solution)/shard_map/ppermute | solution.py:57
  243.8 4.3 %collective-permute-start.6 = (f32[128,128]{1,0:T(8,128)S(1)}, f32[128,128]{1,0:T(8,128)S(1)}, u32[]{:S(2)}, u32[]{:S(2)}) collective-permute-start(f32[128,128]{1,0:T(8,128)S(1)} %add.75), channel_id=1, source_target_pairs={{0,8},{1,9},{2,10},{3,11},{4,12},{5,13},{6,14},{7,15},{8,0},{9,1},... | collective-permute-start | bytes 196616 | tf_op jit(solution)/shard_map/ppermute | solution.py:57
  248.2 5.2 %collective-permute-start.7 = (f32[128,128]{1,0:T(8,128)S(1)}, f32[128,128]{1,0:T(8,128)S(1)}, u32[]{:S(2)}, u32[]{:S(2)}) collective-permute-start(f32[128,128]{1,0:T(8,128)S(1)} %add.76), channel_id=1, source_target_pairs={{0,16},{1,17},{2,18},{3,19},{4,20},{5,21},{6,22},{7,23},{8,24},{9,... | collective-permute-start | bytes 196616 | tf_op jit(solution)/shard_map/ppermute | solution.py:57
Sparse Core Ops, SparseCore 0:
  10.1 75.4 all-gather.1
  144.4 86.8 reduce-scatter.1

commit v9 on v4

--- a/solution.py
+++ b/solution.py
@@ -62,7 +62,7 @@
 def slot_product(blocks, source, block_row, block_col, counts, out_rows, transpose):
     slot_count, block_size = blocks.shape[0], blocks.shape[1]
     width = source.shape[1]
-    group = 32 if slot_count % 32 == 0 else 1
+    group = 64 if slot_count % 64 == 0 else 1
 
     def kernel(row_ref, col_ref, count_ref, block_ref, source_ref, out_ref):
         step = pl.program_id(0)

time: 282 us -> 281 us (level)
  no operation moved by 1% of the time
where the time goes in v9:
time: 281 us
  waiting for transfers between devices  205 us (73%)
  other arithmetic  26.6 us (9%)
  Pallas kernels  17.6 us (6%)
  between operations  14.9 us (5%)
  starting transfers between devices  8.86 us (3%)
  matrix products  3.98 us (1%)
  local copies, waits for them, and re-layouts  3.2 us (1%)
    reduce_scatter x1, waiting for transfers between devices, shards(): lax.psum_scatter(w_partial, 'row', scatter_dimension=0, tiled=True)  86.9 us
    all_gather x1, waiting for transfers between devices, shards(): stripe_probe = lax.all_gather(probe, 'row', axis=0, tiled=True)  76.3 us
    ppermute x1, waiting for transfers between devices, pair_all_reduce(): part = part + lax.ppermute(part, axis, [(i, i ^ step) for i in range(n)])  23.7 us
    pallas_call x2, Pallas kernels, slot_product(): pl.pallas_call(kernel, grid_spec=grid_spec, out_shape=jax.ShapeDtypeStruc...  17.6 us
    ppermute x5, waiting for transfers between devices, butterfly_sum(): x = x + lax.ppermute(x, axes, [(i, i ^ step) for i in range(n)])  12.4 us
    another operation x3, other arithmetic, shards(): lower = jnp.linalg.cholesky(gram)  12.4 us
    another operation x2, other arithmetic, shards(): lax.linalg.triangular_solve(lower, sketch, left_side=False, lower=True, t...  10.5 us
    ppermute x5, starting transfers between devices, butterfly_sum(): x = x + lax.ppermute(x, axes, [(i, i ^ step) for i in range(n)])  7.11 us
  transfers between devices with their start and end apart: 10, of which 10 were waited for; matrix products, arithmetic and copies ran while one was open for 0% of the time, Pallas kernels for 0%

profile of v9, /device:TPU:0, one launch (start us, length us, event | category | flops | bytes accessed | tf_op | source)
XLA Modules:
  0.0 280.6 jit_solution(664129669825244779)
XLA Ops:
  9.3 76.3 %all-gather.2.cloned.1.call-done.source_ref = f32[8192,128]{1,0:T(8,128)} async-done(((f32[1024,128]{1,0:T(8,128)}), f32[8192,128]{1,0:T(8,128)}) %all-gather.2.cloned.1.call-update) | async-done | bytes 4194320 | tf_op jit(solution)/shard_map/all_gather | solution.py:126
  87.0 8.1 %shard_map.77 = f32[4096,128]{1,0:T(8,128)S(1)} custom-call(s32[128]{0:T(128)S(1)} %copy-done, s32[128]{0:T(128)S(1)} %copy-done.2, s32[1]{0:T(128)S(6)} %copy.13.count_ref, f32[128,128,128]{2,1,0:T(8,128)} %block_ref.3, f32[8192,128]{1,0:T(8,128)} %all-gather.2.cloned.1.call-done.source_ref), custom_call_target="tpu_custom_call" | custom-call | tf_op jit(solution)/shard_map/pallas_call | solution.py:103
  95.5 2.8 collective-permute-done
  98.2 1.3 bitcast_add_fusion
  99.6 1.5 collective-permute-start.1
  101.1 23.7 %collective-permute-done.1 = f32[2048,128]{1,0:T(8,128)S(1)} collective-permute-done((f32[2048,128]{1,0:T(8,128)S(1)}, f32[2048,128]{1,0:T(8,128)S(1)}, u32[]{:S(2)}, u32[]{:S(2)}) %collective-permute-start.1) | collective-permute-done | bytes 1048608 | tf_op jit(solution)/shard_map/ppermute | solution.py:46
  125.1 2.6 collective-permute-done.2
  127.7 1.0 copy-done.7
  128.6 2.0 fusion.2
  130.7 9.5 %shard_map.78 = f32[8192,128]{1,0:T(8,128)} custom-call(s32[128]{0:T(128)S(1)} %copy-done.1, s32[128]{0:T(128)S(1)} %copy-done.3, s32[1]{0:T(128)S(6)} %copy.13.count_ref, f32[128,128,128]{2,1,0:T(8,128)} %block_ref.3, f32[4096,128]{1,0:T(8,128)S(1)} %bitcast.17), custom_call_target="tpu_custom_call" | custom-call | tf_op jit(solution)/shard_map/pallas_call | solution.py:103
  140.2 86.9 %reduce-scatter.2.cloned.1.call-done = f32[1024,128]{1,0:T(8,128)} async-done(((f32[8192,128]{1,0:T(8,128)}), f32[1024,128]{1,0:T(8,128)}) %reduce-scatter.2.cloned.1.call-update) | async-done | bytes 524304 | tf_op jit(solution)/shard_map/reduce_scatter | solution.py:139
  227.1 2.6 fusion.3
  229.8 1.2 collective-permute-done.3
  231.0 1.5 collective-permute-start.4
  232.6 2.8 collective-permute-done.4
  235.4 1.5 collective-permute-start.5
  236.9 2.8 collective-permute-done.5
  239.7 1.8 collective-permute-start.6
  241.5 2.5 collective-permute-done.6
  244.1 2.2 collective-permute-start.7
  246.3 3.1 %collective-permute-done.7 = f32[128,128]{0,1:T(8,128)S(1)} collective-permute-done((f32[128,128]{0,1:T(8,128)S(1)}, f32[128,128]{0,1:T(8,128)S(1)}, u32[]{:S(2)}, u32[]{:S(2)}) %collective-permute-start.7) | collective-permute-done | bytes 65568 | tf_op jit(solution)/shard_map/ppermute | solution.py:57
  249.4 11.7 %cholesky.16 = f32[128,128]{1,0:T(8,128)S(1)} custom-call(f32[128,128]{1,0:T(8,128)S(1)} %fusion.6), custom_call_target="Cholesky" | custom-call | tf_op jit(solution)/shard_map/jit(cholesky)/cholesky | solution.py:143
  262.5 9.8 %custom-call.6 = f32[1,128,128]{1,2,0:T(8,128)S(1)} custom-call(f32[1,128,128]{2,1,0:T(8,128)S(1)} %fusion.4), custom_call_target="InvertDiagBlocksLowerTriangular" | custom-call | tf_op jit(solution)/shard_map/triangular_solve | solution.py:144
  272.3 1.4 convolution_multiply_fusion
  (37 shorter events, 5.0 us)
Async XLA Ops:
  7.2 78.5 %all-gather.2.cloned.1.call-start = ((), (), s32[]{:S(2)}) async-start(), calls=%async_computation.1 | async-start | bytes 4718592 | tf_op jit(solution)/shard_map/all_gather | solution.py:126
  7.9 219.2 %reduce-scatter.2.cloned.1.call-start = ((), (), s32[]{:S(2)}) async-start(), calls=%async_computation.2 | async-start | bytes 4718592 | tf_op jit(solution)/shard_map/reduce_scatter | solution.py:139
  85.6 0.7 copy-start
  86.3 0.7 copy-start.2
  87.0 8.1 %copy-start.6 = (f32[1024,128]{1,0:T(8,128)S(1)}, f32[1024,128]{1,0:T(8,128)}, u32[]{:S(2)}) copy-start(f32[1024,128]{1,0:T(8,128)} %param.6) | copy-start | bytes 1572868
  95.4 2.9 %collective-permute-start = (f32[2048,128]{1,0:T(8,128)S(1)}, f32[2048,128]{1,0:T(8,128)}, u32[]{:S(2)}, u32[]{:S(2)}) collective-permute-start(f32[2048,128]{1,0:T(8,128)S(1)} %dynamic-slice_bitcast_fusion), channel_id=1, source_target_pairs={{0,1},{1,0},{2,3},{3,2},{4,5},{5,4},{6,7},{7,6},{8,9},{9,8},{10,11... | collective-permute-start | bytes 3145736 | tf_op jit(solution)/shard_map/ppermute | solution.py:43
  99.6 25.3 %collective-permute-start.1 = (f32[2048,128]{1,0:T(8,128)S(1)}, f32[2048,128]{1,0:T(8,128)S(1)}, u32[]{:S(2)}, u32[]{:S(2)}) collective-permute-start(f32[2048,128]{1,0:T(8,128)S(1)} %bitcast_add_fusion), channel_id=1, source_target_pairs={{0,2},{1,3},{2,0},{3,1},{4,6},{5,7},{6,4},{7,5},{8,10},{9,11},{10,... | collective-permute-start | bytes 3145736 | tf_op jit(solution)/shard_map/ppermute | solution.py:46
  124.9 2.7 collective-permute-start.2
  127.7 1.0 copy-start.7
  128.6 2.0 copy-start.1
  128.6 2.0 copy-start.3
  140.2 133.5 %copy-start.4 = (f32[1024,128]{1,0:T(8,128)}, f32[1024,128]{1,0:T(8,128)S(1)}, u32[]{:S(2)}) copy-start(f32[1024,128]{1,0:T(8,128)S(1)} %constant_dynamic-slice_fusion) | copy-start | bytes 1572868
  227.1 45.2 %copy-start.5 = (f32[1024,128]{1,0:T(8,128)S(1)}, f32[1024,128]{1,0:T(8,128)}, u32[]{:S(2)}) copy-start(f32[1024,128]{1,0:T(8,128)} %reduce-scatter.2.cloned.1.call-done) | copy-start | bytes 1572868
  229.7 1.3 collective-permute-start.3
  231.0 4.3 %collective-permute-start.4 = (f32[128,128]{0,1:T(8,128)S(1)}, f32[128,128]{0,1:T(8,128)S(1)}, u32[]{:S(2)}, u32[]{:S(2)}) collective-permute-start(f32[128,128]{0,1:T(8,128)S(1)} %add.78), channel_id=1, source_target_pairs={{0,2},{1,3},{2,0},{3,1},{4,6},{5,7},{6,4},{7,5},{8,10},{9,11},{10,... | collective-permute-start | bytes 196616 | tf_op jit(solution)/shard_map/ppermute | solution.py:57
  235.4 4.3 %collective-permute-start.5 = (f32[128,128]{0,1:T(8,128)S(1)}, f32[128,128]{0,1:T(8,128)S(1)}, u32[]{:S(2)}, u32[]{:S(2)}) collective-permute-start(f32[128,128]{0,1:T(8,128)S(1)} %add.79), channel_id=1, source_target_pairs={{0,4},{1,5},{2,6},{3,7},{4,0},{5,1},{6,2},{7,3},{8,12},{9,13},{10,... | collective-permute-start | bytes 196616 | tf_op jit(solution)/shard_map/ppermute | solution.py:57
  239.7 4.3 %collective-permute-start.6 = (f32[128,128]{0,1:T(8,128)S(1)}, f32[128,128]{0,1:T(8,128)S(1)}, u32[]{:S(2)}, u32[]{:S(2)}) collective-permute-start(f32[128,128]{0,1:T(8,128)S(1)} %add.80), channel_id=1, source_target_pairs={{0,8},{1,9},{2,10},{3,11},{4,12},{5,13},{6,14},{7,15},{8,0},{9,1},... | collective-permute-start | bytes 196616 | tf_op jit(solution)/shard_map/ppermute | solution.py:57
  244.1 5.2 %collective-permute-start.7 = (f32[128,128]{0,1:T(8,128)S(1)}, f32[128,128]{0,1:T(8,128)S(1)}, u32[]{:S(2)}, u32[]{:S(2)}) collective-permute-start(f32[128,128]{0,1:T(8,128)S(1)} %add.81), channel_id=1, source_target_pairs={{0,16},{1,17},{2,18},{3,19},{4,20},{5,21},{6,22},{7,23},{8,24},{9,... | collective-permute-start | bytes 196616 | tf_op jit(solution)/shard_map/ppermute | solution.py:57
Sparse Core Ops, SparseCore 0:
  10.1 75.4 all-gather.1
  140.3 86.7 reduce-scatter.1

commit v10 on v4

--- a/solution.py
+++ b/solution.py
@@ -35,7 +35,7 @@
 def pair_all_reduce(x, axis, n):
     groups = n // 2
     if n % 2 or groups & (groups - 1):
-        return lax.psum(x, axis)
+        return lax.psum(x, axis), None, 0
     inner = lax.axis_index(axis) % 2
     halves = x.reshape(2, x.shape[0] // 2, *x.shape[1:])
     keep = lax.dynamic_index_in_dim(halves, inner, 0, keepdims=False)
@@ -46,7 +46,7 @@
         part = part + lax.ppermute(part, axis, [(i, i ^ step) for i in range(n)])
         step *= 2
     other = lax.ppermute(part, axis, [(i, i ^ 1) for i in range(n)])
-    return jnp.roll(jnp.stack([part, other]), inner, axis=0).reshape(x.shape)
+    return part, other, inner
 
 
 def butterfly_sum(x, axes, n):
@@ -59,12 +59,16 @@
     return x
 
 
-def slot_product(blocks, source, block_row, block_col, counts, out_rows, transpose):
+def slot_product(blocks, sources, inner, block_row, block_col, counts, out_rows, transpose):
     slot_count, block_size = blocks.shape[0], blocks.shape[1]
-    width = source.shape[1]
+    width = sources[0].shape[1]
+    half_blocks = sources[0].shape[0] // block_size
+    total_blocks = half_blocks * len(sources)
     group = 32 if slot_count % 32 == 0 else 1
 
-    def kernel(row_ref, col_ref, count_ref, block_ref, source_ref, out_ref):
+    def kernel(row_ref, col_ref, count_ref, inner_ref, block_ref, *refs):
+        out_ref = refs[-1]
+        source_refs = refs[:-1]
         step = pl.program_id(0)
 
         @pl.when(step == 0)
@@ -75,10 +79,14 @@
             slot = step * group + s
             read = row_ref[slot] if transpose else col_ref[slot]
             write = col_ref[slot] if transpose else row_ref[slot]
-            read = jnp.clip(read, 0, source_ref.shape[0] // block_size - 1)
+            read = jnp.clip(read, 0, total_blocks - 1)
             write = jnp.clip(write, 0, out_ref.shape[0] // block_size - 1)
             live = (slot < count_ref[0]).astype(jnp.float32)
-            piece = source_ref[pl.ds(pl.multiple_of(read * block_size, block_size), block_size), :]
+            local = read % half_blocks
+            at_read = pl.ds(pl.multiple_of(local * block_size, block_size), block_size)
+            piece = source_refs[0][at_read, :]
+            if len(source_refs) > 1:
+                piece = jnp.where(read // half_blocks == inner_ref[0], piece, source_refs[1][at_read, :])
             block = block_ref[s]
             if transpose:
                 block = block.T
@@ -92,12 +100,12 @@
         lax.fori_loop(0, group, body, 0, unroll=True)
 
     grid_spec = pltpu.PrefetchScalarGridSpec(
-        num_scalar_prefetch=3,
+        num_scalar_prefetch=4,
         grid=(slot_count // group,),
         in_specs=[
             pl.BlockSpec((group, block_size, block_size), lambda g, *_: (g, 0, 0)),
-            pl.BlockSpec(source.shape, lambda g, *_: (0, 0)),
-        ],
+        ]
+        + [pl.BlockSpec(source.shape, lambda g, *_: (0, 0)) for source in sources],
         out_specs=pl.BlockSpec((out_rows, width), lambda g, *_: (0, 0)),
     )
     return pl.pallas_call(
@@ -108,7 +116,7 @@
             dimension_semantics=("arbitrary",), vmem_limit_bytes=48 * 1024 * 1024
         ),
         interpret=INTERPRET,
-    )(block_row, block_col, counts, blocks, source)
+    )(block_row, block_col, counts, inner, blocks, *sources)
 
 
 def shards(probe, self_weight, blocks, block_row, block_col, counts):
@@ -125,7 +133,8 @@
     answers = local_rows * row_count * col_count
     stripe_probe = lax.all_gather(probe, "row", axis=0, tiled=True)
     partial_value = slot_product(
-        blocks, stripe_probe, block_row, block_col, counts, owner_rows, False
+        blocks, (stripe_probe,), jnp.zeros((1,), jnp.int32), block_row, block_col, counts,
+        owner_rows, False,
     )
     local_start = lax.axis_index("col") * local_rows
     local_weight = lax.dynamic_slice_in_dim(self_weight, local_start, local_rows, 0)
@@ -133,9 +142,23 @@
     partial_value = lax.dynamic_update_slice_in_dim(
         partial_value, own_rows + local_weight[:, None] * probe, local_start, 0
     )
-    owner_y = pair_all_reduce(partial_value, "col", col_count)
-    projected = lax.dynamic_slice_in_dim(owner_y, local_start, local_rows, 0)
-    w_partial = slot_product(blocks, owner_y, block_row, block_col, counts, stripe_rows, True)
+    part, other, inner = pair_all_reduce(partial_value, "col", col_count)
+    inner = jnp.reshape(inner, (1,)).astype(jnp.int32)
+    if other is None:
+        sources = (part,)
+        projected = lax.dynamic_slice_in_dim(part, local_start, local_rows, 0)
+    else:
+        sources = (part, other)
+        half_rows = part.shape[0]
+        offset = local_start % half_rows
+        projected = jnp.where(
+            local_start // half_rows == inner[0],
+            lax.dynamic_slice_in_dim(part, offset, local_rows, 0),
+            lax.dynamic_slice_in_dim(other, offset, local_rows, 0),
+        )
+    w_partial = slot_product(
+        blocks, sources, inner, block_row, block_col, counts, stripe_rows, True
+    )
     w_share = lax.psum_scatter(w_partial, "row", scatter_dimension=0, tiled=True)
     sketch = local_weight[:, None] * projected + w_share
     gram_part = jnp.dot(sketch.T, sketch, precision=PRECISE, preferred_element_type=jnp.float32)

time: 282 us -> 279 us (0.989)
  no operation moved by 1% of the time
where the time goes in v10:
time: 279 us; the launch traced here: 278 us
  waiting for transfers between devices  205 us (73%)
  other arithmetic  24.6 us (9%)
  Pallas kernels  18.3 us (7%)
  between operations  14.9 us (5%)
  starting transfers between devices  8.89 us (3%)
  matrix products  3.98 us (1%)
    reduce_scatter x1, waiting for transfers between devices, shards(): lax.psum_scatter(w_partial, 'row', scatter_dimension=0, tiled=True)  86.9 us
    all_gather x1, waiting for transfers between devices, shards(): stripe_probe = lax.all_gather(probe, 'row', axis=0, tiled=True)  76.3 us
    ppermute x1, waiting for transfers between devices, pair_all_reduce(): part = part + lax.ppermute(part, axis, [(i, i ^ step) for i in range(n)])  23.7 us
    pallas_call x2, Pallas kernels, slot_product(): pl.pallas_call(kernel, grid_spec=grid_spec, out_shape=jax.ShapeDtypeStruc...  18.3 us
    ppermute x5, waiting for transfers between devices, butterfly_sum(): x = x + lax.ppermute(x, axes, [(i, i ^ step) for i in range(n)])  12.4 us
    another operation x3, other arithmetic, shards(): lower = jnp.linalg.cholesky(gram)  12.4 us
    another operation x2, other arithmetic, shards(): lax.linalg.triangular_solve(lower, sketch, left_side=False, lower=True, t...  10.5 us
    ppermute x5, starting transfers between devices, butterfly_sum(): x = x + lax.ppermute(x, axes, [(i, i ^ step) for i in range(n)])  7.14 us
  transfers between devices with their start and end apart: 10, of which 10 were waited for; matrix products, arithmetic and copies ran while one was open for 0% of the time, Pallas kernels for 0%

profile of v10, /device:TPU:0, one launch (start us, length us, event | category | flops | bytes accessed | tf_op | source)
XLA Modules:
  0.0 278.3 jit_solution(1248598840535049159)
XLA Ops:
  7.2 0.7 all-gather.2.cloned.1.call-update
  8.6 0.7 dynamic_slice.20
  9.3 76.3 %all-gather.2.cloned.1.call-done.refs_0_ = f32[8192,128]{1,0:T(8,128)} async-done(((f32[1024,128]{1,0:T(8,128)}), f32[8192,128]{1,0:T(8,128)}) %all-gather.2.cloned.1.call-update) | async-done | bytes 4194320 | tf_op jit(solution)/shard_map/all_gather | solution.py:134
  87.0 8.5 %shard_map.77 = f32[4096,128]{1,0:T(8,128)S(1)} custom-call(s32[128]{0:T(128)S(1)} %copy-done, s32[128]{0:T(128)S(1)} %copy-done.2, s32[1]{0:T(128)S(6)} %copy.13.count_ref, s32[1]{0:T(128)} %constant.89.clone.1.inner_ref, f32[128,128,128]{2,1,0:T(8,128)} %block_ref.3, f32[8192,128]{1,0:T(8,128)} %all-gather.2.cloned.1.call-done.refs_0_), custom_call_target="tpu_custom_call" | custom-call | tf_op jit(solution)/shard_map/pallas_call | solution.py:111
  95.9 2.8 collective-permute-done
  98.7 1.3 bitcast_add_fusion
  100.0 1.5 collective-permute-start.1
  101.6 23.7 %collective-permute-done.1 = f32[2048,128]{1,0:T(8,128)S(1)} collective-permute-done((f32[2048,128]{1,0:T(8,128)S(1)}, f32[2048,128]{1,0:T(8,128)S(1)}, u32[]{:S(2)}, u32[]{:S(2)}) %collective-permute-start.1) | collective-permute-done | bytes 1048608 | tf_op jit(solution)/shard_map/ppermute | solution.py:46
  125.5 2.6 collective-permute-done.2.refs_1_
  128.1 9.7 %shard_map.78 = f32[8192,128]{1,0:T(8,128)} custom-call(s32[128]{0:T(128)S(1)} %copy-done.1, s32[128]{0:T(128)S(1)} %copy-done.3, s32[1]{0:T(128)S(6)} %copy.13.count_ref, s32[1]{0:T(128)} %bitcast.3.inner_ref, f32[128,128,128]{2,1,0:T(8,128)} %block_ref.3, f32[2048,128]{1,0:T(8,128)S(1)} %add.71.refs_0_, f32[2048,128]{1,0:T(8,128)S(1)} %collective-permute-done.2.refs_1_), custom_call_target="tpu_custom_call" | custom-call | tf_op jit(solution)/shard_map/pallas_call | solution.py:111
  138.0 86.9 %reduce-scatter.2.cloned.1.call-done = f32[1024,128]{1,0:T(8,128)} async-done(((f32[8192,128]{1,0:T(8,128)}), f32[1024,128]{1,0:T(8,128)}) %reduce-scatter.2.cloned.1.call-update) | async-done | bytes 524304 | tf_op jit(solution)/shard_map/reduce_scatter | solution.py:162
  224.9 2.6 fusion
  227.5 1.2 collective-permute-done.3
  228.8 1.5 collective-permute-start.4
  230.3 2.8 %collective-permute-done.4 = f32[128,128]{0,1:T(8,128)S(1)} collective-permute-done((f32[128,128]{0,1:T(8,128)S(1)}, f32[128,128]{0,1:T(8,128)S(1)}, u32[]{:S(2)}, u32[]{:S(2)}) %collective-permute-start.4) | collective-permute-done | bytes 65568 | tf_op jit(solution)/shard_map/ppermute | solution.py:57
  233.1 1.5 collective-permute-start.5
  234.7 2.8 %collective-permute-done.5 = f32[128,128]{0,1:T(8,128)S(1)} collective-permute-done((f32[128,128]{0,1:T(8,128)S(1)}, f32[128,128]{0,1:T(8,128)S(1)}, u32[]{:S(2)}, u32[]{:S(2)}) %collective-permute-start.5) | collective-permute-done | bytes 65568 | tf_op jit(solution)/shard_map/ppermute | solution.py:57
  237.5 1.8 collective-permute-start.6
  239.2 2.6 collective-permute-done.6
  241.8 2.2 collective-permute-start.7
  244.1 3.0 %collective-permute-done.7 = f32[128,128]{0,1:T(8,128)S(1)} collective-permute-done((f32[128,128]{0,1:T(8,128)S(1)}, f32[128,128]{0,1:T(8,128)S(1)}, u32[]{:S(2)}, u32[]{:S(2)}) %collective-permute-start.7) | collective-permute-done | bytes 65568 | tf_op jit(solution)/shard_map/ppermute | solution.py:57
  247.2 11.7 %cholesky.16 = f32[128,128]{1,0:T(8,128)S(1)} custom-call(f32[128,128]{1,0:T(8,128)S(1)} %fusion.3), custom_call_target="Cholesky" | custom-call | tf_op jit(solution)/shard_map/jit(cholesky)/cholesky | solution.py:166
  260.2 9.8 %custom-call.6 = f32[1,128,128]{1,2,0:T(8,128)S(1)} custom-call(f32[1,128,128]{2,1,0:T(8,128)S(1)} %fusion.1), custom_call_target="InvertDiagBlocksLowerTriangular" | custom-call | tf_op jit(solution)/shard_map/triangular_solve | solution.py:167
  270.1 1.4 convolution_multiply_fusion
  (34 shorter events, 3.6 us)
Async XLA Ops:
  7.2 78.5 %all-gather.2.cloned.1.call-start = ((), (), s32[]{:S(2)}) async-start(), calls=%async_computation.1 | async-start | bytes 4718592 | tf_op jit(solution)/shard_map/all_gather | solution.py:134
  7.9 217.0 %reduce-scatter.2.cloned.1.call-start = ((), (), s32[]{:S(2)}) async-start(), calls=%async_computation.2 | async-start | bytes 4718592 | tf_op jit(solution)/shard_map/reduce_scatter | solution.py:162
  85.6 0.7 copy-start
  86.3 0.7 copy-start.2
  87.0 8.5 %copy-start.6 = (f32[1024,128]{1,0:T(8,128)S(1)}, f32[1024,128]{1,0:T(8,128)}, u32[]{:S(2)}) copy-start(f32[1024,128]{1,0:T(8,128)} %param.6) | copy-start | bytes 1572868
  95.8 2.9 %collective-permute-start = (f32[2048,128]{1,0:T(8,128)S(1)}, f32[2048,128]{1,0:T(8,128)}, u32[]{:S(2)}, u32[]{:S(2)}) collective-permute-start(f32[2048,128]{1,0:T(8,128)S(1)} %dynamic-slice_bitcast_fusion), channel_id=1, source_target_pairs={{0,1},{1,0},{2,3},{3,2},{4,5},{5,4},{6,7},{7,6},{8,9},{9,8},{10,11... | collective-permute-start | bytes 3145736 | tf_op jit(solution)/shard_map/ppermute | solution.py:43
  100.0 28.1 %copy-start.1 = (s32[128]{0:T(128)S(1)}, s32[128]{0:T(128)}, u32[]{:S(2)}) copy-start(s32[128]{0:T(128)} %row_ref.3) | copy-start | bytes 1540
  100.0 28.1 %copy-start.3 = (s32[128]{0:T(128)S(1)}, s32[128]{0:T(128)}, u32[]{:S(2)}) copy-start(s32[128]{0:T(128)} %col_ref.3) | copy-start | bytes 1540
  100.0 25.3 %collective-permute-start.1 = (f32[2048,128]{1,0:T(8,128)S(1)}, f32[2048,128]{1,0:T(8,128)S(1)}, u32[]{:S(2)}, u32[]{:S(2)}) collective-permute-start(f32[2048,128]{1,0:T(8,128)S(1)} %bitcast_add_fusion), channel_id=1, source_target_pairs={{0,2},{1,3},{2,0},{3,1},{4,6},{5,7},{6,4},{7,5},{8,10},{9,11},{10,... | collective-permute-start | bytes 3145736 | tf_op jit(solution)/shard_map/ppermute | solution.py:46
  125.4 2.7 collective-permute-start.2
  138.0 133.5 %copy-start.4 = (f32[1024,128]{1,0:T(8,128)}, f32[1024,128]{1,0:T(8,128)S(1)}, u32[]{:S(2)}) copy-start(f32[1024,128]{1,0:T(8,128)S(1)} %dynamic-slice_select_fusion) | copy-start | bytes 1572868
  224.9 45.2 %copy-start.5 = (f32[1024,128]{1,0:T(8,128)S(1)}, f32[1024,128]{1,0:T(8,128)}, u32[]{:S(2)}) copy-start(f32[1024,128]{1,0:T(8,128)} %reduce-scatter.2.cloned.1.call-done) | copy-start | bytes 1572868
  227.5 1.3 collective-permute-start.3
  228.8 4.3 %collective-permute-start.4 = (f32[128,128]{0,1:T(8,128)S(1)}, f32[128,128]{0,1:T(8,128)S(1)}, u32[]{:S(2)}, u32[]{:S(2)}) collective-permute-start(f32[128,128]{0,1:T(8,128)S(1)} %add.75), channel_id=1, source_target_pairs={{0,2},{1,3},{2,0},{3,1},{4,6},{5,7},{6,4},{7,5},{8,10},{9,11},{10,... | collective-permute-start | bytes 196616 | tf_op jit(solution)/shard_map/ppermute | solution.py:57
  233.1 4.3 %collective-permute-start.5 = (f32[128,128]{0,1:T(8,128)S(1)}, f32[128,128]{0,1:T(8,128)S(1)}, u32[]{:S(2)}, u32[]{:S(2)}) collective-permute-start(f32[128,128]{0,1:T(8,128)S(1)} %add.76), channel_id=1, source_target_pairs={{0,4},{1,5},{2,6},{3,7},{4,0},{5,1},{6,2},{7,3},{8,12},{9,13},{10,... | collective-permute-start | bytes 196616 | tf_op jit(solution)/shard_map/ppermute | solution.py:57
  237.5 4.3 %collective-permute-start.6 = (f32[128,128]{0,1:T(8,128)S(1)}, f32[128,128]{0,1:T(8,128)S(1)}, u32[]{:S(2)}, u32[]{:S(2)}) collective-permute-start(f32[128,128]{0,1:T(8,128)S(1)} %add.77), channel_id=1, source_target_pairs={{0,8},{1,9},{2,10},{3,11},{4,12},{5,13},{6,14},{7,15},{8,0},{9,1},... | collective-permute-start | bytes 196616 | tf_op jit(solution)/shard_map/ppermute | solution.py:57
  241.8 5.2 %collective-permute-start.7 = (f32[128,128]{0,1:T(8,128)S(1)}, f32[128,128]{0,1:T(8,128)S(1)}, u32[]{:S(2)}, u32[]{:S(2)}) collective-permute-start(f32[128,128]{0,1:T(8,128)S(1)} %add.78), channel_id=1, source_target_pairs={{0,16},{1,17},{2,18},{3,19},{4,20},{5,21},{6,22},{7,23},{8,24},{9,... | collective-permute-start | bytes 196616 | tf_op jit(solution)/shard_map/ppermute | solution.py:57
Sparse Core Ops, SparseCore 0:
  10.1 75.4 all-gather.1
  138.0 86.8 reduce-scatter.1

commit v11 on v10

--- a/solution.py
+++ b/solution.py
@@ -64,7 +64,7 @@
     width = sources[0].shape[1]
     half_blocks = sources[0].shape[0] // block_size
     total_blocks = half_blocks * len(sources)
-    group = 32 if slot_count % 32 == 0 else 1
+    group = 64 if slot_count % 64 == 0 else 1
 
     def kernel(row_ref, col_ref, count_ref, inner_ref, block_ref, *refs):
         out_ref = refs[-1]

time: 279 us -> 278 us (level)
  no operation moved by 1% of the time
where the time goes in v11:
time: 278 us
  waiting for transfers between devices  206 us (74%)
  other arithmetic  24.6 us (9%)
  Pallas kernels  17.7 us (6%)
  between operations  14.9 us (5%)
  starting transfers between devices  8.85 us (3%)
  matrix products  3.97 us (1%)
    reduce_scatter x1, waiting for transfers between devices, shards(): lax.psum_scatter(w_partial, 'row', scatter_dimension=0, tiled=True)  86.9 us
    all_gather x1, waiting for transfers between devices, shards(): stripe_probe = lax.all_gather(probe, 'row', axis=0, tiled=True)  76.3 us
    ppermute x1, waiting for transfers between devices, pair_all_reduce(): part = part + lax.ppermute(part, axis, [(i, i ^ step) for i in range(n)])  23.7 us
    pallas_call x2, Pallas kernels, slot_product(): pl.pallas_call(kernel, grid_spec=grid_spec, out_shape=jax.ShapeDtypeStruc...  17.7 us
    ppermute x5, waiting for transfers between devices, butterfly_sum(): x = x + lax.ppermute(x, axes, [(i, i ^ step) for i in range(n)])  12.4 us
    another operation x3, other arithmetic, shards(): lower = jnp.linalg.cholesky(gram)  12.4 us
    another operation x2, other arithmetic, shards(): lax.linalg.triangular_solve(lower, sketch, left_side=False, lower=True, t...  10.5 us
    ppermute x5, starting transfers between devices, butterfly_sum(): x = x + lax.ppermute(x, axes, [(i, i ^ step) for i in range(n)])  7.09 us
  transfers between devices with their start and end apart: 10, of which 10 were waited for; matrix products, arithmetic and copies ran while one was open for 0% of the time, Pallas kernels for 0%

profile of v11, /device:TPU:0, one launch (start us, length us, event | category | flops | bytes accessed | tf_op | source)
XLA Modules:
  0.0 277.8 jit_solution(15044157966463803696)
XLA Ops:
  7.2 0.7 all-gather.2.cloned.1.call-update
  8.6 0.7 dynamic_slice.20
  9.3 76.3 %all-gather.2.cloned.1.call-done.refs_0_ = f32[8192,128]{1,0:T(8,128)} async-done(((f32[1024,128]{1,0:T(8,128)}), f32[8192,128]{1,0:T(8,128)}) %all-gather.2.cloned.1.call-update) | async-done | bytes 4194320 | tf_op jit(solution)/shard_map/all_gather | solution.py:134
  87.0 8.2 %shard_map.77 = f32[4096,128]{1,0:T(8,128)S(1)} custom-call(s32[128]{0:T(128)S(1)} %copy-done, s32[128]{0:T(128)S(1)} %copy-done.2, s32[1]{0:T(128)S(6)} %copy.13.count_ref, s32[1]{0:T(128)} %constant.89.clone.1.inner_ref, f32[128,128,128]{2,1,0:T(8,128)} %block_ref.3, f32[8192,128]{1,0:T(8,128)} %all-gather.2.cloned.1.call-done.refs_0_), custom_call_target="tpu_custom_call" | custom-call | tf_op jit(solution)/shard_map/pallas_call | solution.py:111
  95.6 2.8 collective-permute-done
  98.4 1.3 bitcast_add_fusion
  99.7 1.5 collective-permute-start.1
  101.3 23.7 %collective-permute-done.1 = f32[2048,128]{1,0:T(8,128)S(1)} collective-permute-done((f32[2048,128]{1,0:T(8,128)S(1)}, f32[2048,128]{1,0:T(8,128)S(1)}, u32[]{:S(2)}, u32[]{:S(2)}) %collective-permute-start.1) | collective-permute-done | bytes 1048608 | tf_op jit(solution)/shard_map/ppermute | solution.py:46
  125.2 2.6 collective-permute-done.2.refs_1_
  127.8 9.5 %shard_map.78 = f32[8192,128]{1,0:T(8,128)} custom-call(s32[128]{0:T(128)S(1)} %copy-done.1, s32[128]{0:T(128)S(1)} %copy-done.3, s32[1]{0:T(128)S(6)} %copy.13.count_ref, s32[1]{0:T(128)} %bitcast.3.inner_ref, f32[128,128,128]{2,1,0:T(8,128)} %block_ref.3, f32[2048,128]{1,0:T(8,128)S(1)} %add.71.refs_0_, f32[2048,128]{1,0:T(8,128)S(1)} %collective-permute-done.2.refs_1_), custom_call_target="tpu_custom_call" | custom-call | tf_op jit(solution)/shard_map/pallas_call | solution.py:111
  137.5 86.9 %reduce-scatter.2.cloned.1.call-done = f32[1024,128]{1,0:T(8,128)} async-done(((f32[8192,128]{1,0:T(8,128)}), f32[1024,128]{1,0:T(8,128)}) %reduce-scatter.2.cloned.1.call-update) | async-done | bytes 524304 | tf_op jit(solution)/shard_map/reduce_scatter | solution.py:162
  224.4 2.6 fusion
  227.0 1.2 collective-permute-done.3
  228.3 1.5 collective-permute-start.4
  229.8 2.8 %collective-permute-done.4 = f32[128,128]{0,1:T(8,128)S(1)} collective-permute-done((f32[128,128]{0,1:T(8,128)S(1)}, f32[128,128]{0,1:T(8,128)S(1)}, u32[]{:S(2)}, u32[]{:S(2)}) %collective-permute-start.4) | collective-permute-done | bytes 65568 | tf_op jit(solution)/shard_map/ppermute | solution.py:57
  232.6 1.5 collective-permute-start.5
  234.2 2.8 %collective-permute-done.5 = f32[128,128]{0,1:T(8,128)S(1)} collective-permute-done((f32[128,128]{0,1:T(8,128)S(1)}, f32[128,128]{0,1:T(8,128)S(1)}, u32[]{:S(2)}, u32[]{:S(2)}) %collective-permute-start.5) | collective-permute-done | bytes 65568 | tf_op jit(solution)/shard_map/ppermute | solution.py:57
  237.0 1.7 collective-permute-start.6
  238.7 2.6 collective-permute-done.6
  241.3 2.2 collective-permute-start.7
  243.5 3.0 %collective-permute-done.7 = f32[128,128]{0,1:T(8,128)S(1)} collective-permute-done((f32[128,128]{0,1:T(8,128)S(1)}, f32[128,128]{0,1:T(8,128)S(1)}, u32[]{:S(2)}, u32[]{:S(2)}) %collective-permute-start.7) | collective-permute-done | bytes 65568 | tf_op jit(solution)/shard_map/ppermute | solution.py:57
  246.7 11.7 %cholesky.16 = f32[128,128]{1,0:T(8,128)S(1)} custom-call(f32[128,128]{1,0:T(8,128)S(1)} %fusion.3), custom_call_target="Cholesky" | custom-call | tf_op jit(solution)/shard_map/jit(cholesky)/cholesky | solution.py:166
  259.7 9.8 %custom-call.6 = f32[1,128,128]{1,2,0:T(8,128)S(1)} custom-call(f32[1,128,128]{2,1,0:T(8,128)S(1)} %fusion.1), custom_call_target="InvertDiagBlocksLowerTriangular" | custom-call | tf_op jit(solution)/shard_map/triangular_solve | solution.py:167
  269.6 1.4 convolution_multiply_fusion
  (34 shorter events, 3.6 us)
Async XLA Ops:
  7.2 78.5 %all-gather.2.cloned.1.call-start = ((), (), s32[]{:S(2)}) async-start(), calls=%async_computation.1 | async-start | bytes 4718592 | tf_op jit(solution)/shard_map/all_gather | solution.py:134
  7.9 216.5 %reduce-scatter.2.cloned.1.call-start = ((), (), s32[]{:S(2)}) async-start(), calls=%async_computation.2 | async-start | bytes 4718592 | tf_op jit(solution)/shard_map/reduce_scatter | solution.py:162
  85.6 0.7 copy-start
  86.3 0.7 copy-start.2
  87.0 8.2 %copy-start.6 = (f32[1024,128]{1,0:T(8,128)S(1)}, f32[1024,128]{1,0:T(8,128)}, u32[]{:S(2)}) copy-start(f32[1024,128]{1,0:T(8,128)} %param.6) | copy-start | bytes 1572868
  95.5 2.9 %collective-permute-start = (f32[2048,128]{1,0:T(8,128)S(1)}, f32[2048,128]{1,0:T(8,128)}, u32[]{:S(2)}, u32[]{:S(2)}) collective-permute-start(f32[2048,128]{1,0:T(8,128)S(1)} %dynamic-slice_bitcast_fusion), channel_id=1, source_target_pairs={{0,1},{1,0},{2,3},{3,2},{4,5},{5,4},{6,7},{7,6},{8,9},{9,8},{10,11... | collective-permute-start | bytes 3145736 | tf_op jit(solution)/shard_map/ppermute | solution.py:43
  99.7 28.1 %copy-start.1 = (s32[128]{0:T(128)S(1)}, s32[128]{0:T(128)}, u32[]{:S(2)}) copy-start(s32[128]{0:T(128)} %row_ref.3) | copy-start | bytes 1540
  99.7 28.1 %copy-start.3 = (s32[128]{0:T(128)S(1)}, s32[128]{0:T(128)}, u32[]{:S(2)}) copy-start(s32[128]{0:T(128)} %col_ref.3) | copy-start | bytes 1540
  99.7 25.3 %collective-permute-start.1 = (f32[2048,128]{1,0:T(8,128)S(1)}, f32[2048,128]{1,0:T(8,128)S(1)}, u32[]{:S(2)}, u32[]{:S(2)}) collective-permute-start(f32[2048,128]{1,0:T(8,128)S(1)} %bitcast_add_fusion), channel_id=1, source_target_pairs={{0,2},{1,3},{2,0},{3,1},{4,6},{5,7},{6,4},{7,5},{8,10},{9,11},{10,... | collective-permute-start | bytes 3145736 | tf_op jit(solution)/shard_map/ppermute | solution.py:46
  125.1 2.7 collective-permute-start.2
  137.5 133.5 %copy-start.4 = (f32[1024,128]{1,0:T(8,128)}, f32[1024,128]{1,0:T(8,128)S(1)}, u32[]{:S(2)}) copy-start(f32[1024,128]{1,0:T(8,128)S(1)} %dynamic-slice_select_fusion) | copy-start | bytes 1572868
  224.4 45.2 %copy-start.5 = (f32[1024,128]{1,0:T(8,128)S(1)}, f32[1024,128]{1,0:T(8,128)}, u32[]{:S(2)}) copy-start(f32[1024,128]{1,0:T(8,128)} %reduce-scatter.2.cloned.1.call-done) | copy-start | bytes 1572868
  227.0 1.3 collective-permute-start.3
  228.3 4.3 %collective-permute-start.4 = (f32[128,128]{0,1:T(8,128)S(1)}, f32[128,128]{0,1:T(8,128)S(1)}, u32[]{:S(2)}, u32[]{:S(2)}) collective-permute-start(f32[128,128]{0,1:T(8,128)S(1)} %add.75), channel_id=1, source_target_pairs={{0,2},{1,3},{2,0},{3,1},{4,6},{5,7},{6,4},{7,5},{8,10},{9,11},{10,... | collective-permute-start | bytes 196616 | tf_op jit(solution)/shard_map/ppermute | solution.py:57
  232.6 4.3 %collective-permute-start.5 = (f32[128,128]{0,1:T(8,128)S(1)}, f32[128,128]{0,1:T(8,128)S(1)}, u32[]{:S(2)}, u32[]{:S(2)}) collective-permute-start(f32[128,128]{0,1:T(8,128)S(1)} %add.76), channel_id=1, source_target_pairs={{0,4},{1,5},{2,6},{3,7},{4,0},{5,1},{6,2},{7,3},{8,12},{9,13},{10,... | collective-permute-start | bytes 196616 | tf_op jit(solution)/shard_map/ppermute | solution.py:57
  237.0 4.3 %collective-permute-start.6 = (f32[128,128]{0,1:T(8,128)S(1)}, f32[128,128]{0,1:T(8,128)S(1)}, u32[]{:S(2)}, u32[]{:S(2)}) collective-permute-start(f32[128,128]{0,1:T(8,128)S(1)} %add.77), channel_id=1, source_target_pairs={{0,8},{1,9},{2,10},{3,11},{4,12},{5,13},{6,14},{7,15},{8,0},{9,1},... | collective-permute-start | bytes 196616 | tf_op jit(solution)/shard_map/ppermute | solution.py:57
  241.3 5.2 %collective-permute-start.7 = (f32[128,128]{0,1:T(8,128)S(1)}, f32[128,128]{0,1:T(8,128)S(1)}, u32[]{:S(2)}, u32[]{:S(2)}) collective-permute-start(f32[128,128]{0,1:T(8,128)S(1)} %add.78), channel_id=1, source_target_pairs={{0,16},{1,17},{2,18},{3,19},{4,20},{5,21},{6,22},{7,23},{8,24},{9,... | collective-permute-start | bytes 196616 | tf_op jit(solution)/shard_map/ppermute | solution.py:57
Sparse Core Ops, SparseCore 0:
  10.1 75.4 all-gather.1
  137.5 86.8 reduce-scatter.1
